TPU v7x, 1024 devices: a whole 4x8x16 slice. The times are simulated.
1024 devices in a mesh: domain: 32 (over z, x_lo), band: 32 (over y, x_hi, core).
Axes of the slice: x: 4 (x_hi: 2, x_lo: 2; x = x_hi * 2 + x_lo), y: 8, z: 16, core: 2. Of those that a mesh axis runs over, the one named last changes fastest.
Arguments:
- orbitals: float32 [96, 192, 16, 128], P('band', 'domain'), may hold values from -8.8 to 8.8
- potential: float32 [192, 16, 128], P('domain', None, 'band'), may hold values from -1.5 to 0
Outputs:
- filtered: float32 [96, 192, 16, 128], P('band', 'domain')
- intersection: float32 [96, 96], P('band')
- hamiltonian: float32 [96, 96], P('band')
All inputs are finite; a program needn't handle non-finite values.
Results may differ from a plain program's by a relative error of at most 0.00005.
Values sent between devices are 32-bit elements; how exact they have to be, the bound alone decides.
No kernel may reach another device: no remote copies, remote signals or barrier semaphores. Data moves between devices by JAX's collectives and lax.ppermute only.
A program may use at most 32 MiB of HBM per device.

v0:
```python
import jax
import jax.numpy as jnp
from jax import lax
from jax.sharding import PartitionSpec as P

DEGREE = 8


stencil_coeffs = (
    -5369.0 / 1800.0,
    12.0 / 7.0,
    -15.0 / 56.0,
    10.0 / 189.0,
    -1.0 / 112.0,
    2.0 / 1925.0,
    -1.0 / 16632.0,
)
stencil_reach = 6
lower_bound = 4.5
upper_bound = 15.5
lowest_bound = 1.0


def extended(cells, sides, width):
    for axis, dim in sides:
        count = lax.axis_size(axis)
        head = lax.slice_in_dim(cells, 0, width, axis=dim)
        tail = lax.slice_in_dim(cells, cells.shape[dim] - width, cells.shape[dim], axis=dim)
        cells = jnp.concatenate(
            [
                lax.ppermute(tail, axis, [(i, (i + 1) % count) for i in range(count)]),
                cells,
                lax.ppermute(head, axis, [((i + 1) % count, i) for i in range(count)]),
            ],
            axis=dim,
        )
    return cells


def laplace(grid_field):
    planes = grid_field.shape[1]
    size_y = grid_field.shape[2]
    size_z = grid_field.shape[3]
    padded_x = extended(grid_field, (("domain", 1),), 6)
    padded_yz = jnp.pad(
        grid_field, ((0, 0), (0, 0), (stencil_reach, stencil_reach), (stencil_reach, stencil_reach))
    )
    summed = 3.0 * stencil_coeffs[0] * grid_field
    for offset in range(1, stencil_reach + 1):
        along_x = (
            padded_x[:, stencil_reach + offset : stencil_reach + offset + planes]
            + padded_x[:, stencil_reach - offset : stencil_reach - offset + planes]
        )
        along_y = (
            padded_yz[
                :,
                :,
                stencil_reach + offset : stencil_reach + offset + size_y,
                stencil_reach : stencil_reach + size_z,
            ]
            + padded_yz[
                :,
                :,
                stencil_reach - offset : stencil_reach - offset + size_y,
                stencil_reach : stencil_reach + size_z,
            ]
        )
        along_z = (
            padded_yz[
                :,
                :,
                stencil_reach : stencil_reach + size_y,
                stencil_reach + offset : stencil_reach + offset + size_z,
            ]
            + padded_yz[
                :,
                :,
                stencil_reach : stencil_reach + size_y,
                stencil_reach - offset : stencil_reach - offset + size_z,
            ]
        )
        summed = summed + stencil_coeffs[offset] * (along_x + along_y + along_z)
    return summed


def apply_hamiltonian(grid_field, local_pot):
    return -0.5 * laplace(grid_field) + local_pot[None] * grid_field


def contract(left, right):
    return lax.dot_general(
        left,
        right,
        (((1,), (1,)), ((), ())),
        precision=lax.Precision.HIGHEST,
        preferred_element_type=jnp.float32,
    )


def body(orbitals, potential):
    local_pot = lax.all_gather(potential, "band", axis=2, tiled=True)
    half_width = (upper_bound - lower_bound) / 2.0
    centre = (upper_bound + lower_bound) / 2.0
    sigma_first = half_width / (lowest_bound - centre)
    previous = orbitals
    current = (apply_hamiltonian(previous, local_pot) - centre * previous) * (
        sigma_first / half_width
    )
    sigma_now = sigma_first
    for degree_step in range(2, DEGREE + 1):
        sigma_next = 1.0 / (2.0 / sigma_first - sigma_now)
        update = (apply_hamiltonian(current, local_pot) - centre * current) * (
            2.0 * sigma_next / half_width
        ) - sigma_now * sigma_next * previous
        previous = current
        current = update
        sigma_now = sigma_next
    h_image = apply_hamiltonian(current, local_pot)
    orb_dev = current.shape[0]
    cell_count = current.shape[1] * current.shape[2] * current.shape[3] * lax.axis_size("domain")
    flat_panel = current.reshape(orb_dev, -1)
    flat_image = h_image.reshape(orb_dev, -1)
    panel_in = lax.all_gather(flat_panel, "band", axis=0, tiled=True)
    s_part = contract(flat_panel, panel_in)
    h_part = contract(flat_image, panel_in)
    s_total, h_total = lax.psum((s_part, h_part), "domain")
    intersection = s_total / cell_count
    hamiltonian = h_total / cell_count
    return (current, intersection, hamiltonian)


def solution(mesh):
    placed = (P("band", "domain", None, None), P("domain", None, "band"))
    return jax.shard_map(
        body,
        mesh=mesh,
        in_specs=placed,
        out_specs=(P("band", "domain", None, None), P("band", None), P("band", None)),
        check_vma=False,
    )
```

profile of v0, /device:TPU:8, one launch (start us, length us, event | category | flops | bytes accessed | tf_op | source)
XLA Modules:
  0.0 362.3 jit_solution(6046995976173173333)
XLA Ops:
  7.2 3.4 collective-permute-start.1
  10.6 17.7 %collective-permute-start = (f32[3,6,16,128]{3,2,1,0:T(8,128)}, f32[3,6,16,128]{3,2,1,0:T(8,128)S(1)}, u32[]{:S(2)}, u32[]{:S(2)}) collective-permute-start(f32[3,6,16,128]{3,2,1,0:T(8,128)} %param.2), channel_id=1, source_target_pairs={{32,0},{64,32},{96,64},{128,96},{160,128},{192,160},{224,192},{256... | collective-permute-start | bytes 442376 | tf_op jit(solution)/shard_map/ppermute | solution.py:33
  29.0 41.2 %all_gather.6 = f32[6,16,128]{1,0,2:T(8,128)S(1)} all-gather(f32[6,16,4]{1,0,2:T(8,128)S(1)} %copy.12), channel_id=1, replica_groups=mesh['domain'=32,'band'=32] {'band'}, dimensions={2}, use_global_device_ids=true | all-gather | bytes 50688 | tf_op jit(solution)/shard_map/all_gather | solution.py:101
  71.3 4.9 %broadcast_multiply_fusion = (f32[3,6,16,128]{3,2,1,0:T(8,128)S(1)}, f32[3,6,16,128]{3,2,1,0:T(8,128)S(1)}) fusion(f32[3,6,16,128]{3,2,1,0:T(8,128)} %param.2, f32[6,16,128]{2,1,0:T(8,128)S(1)} %copy.13, f32[3,6,16,128]{3,2,1,0:T(8,128)S(1)} %collective-permute-done, f32[3,6,16,128]{3,2,1,0:T(8,128)S(1)} %collective-permute-done.1, ...), kind=kLoop, calls=%fused_computation.839 | loop fusion | flops 1806336 | bytes 2260992 | tf_op jit(solution)/shard_map/mul | solution.py:106
  78.1 6.0 %collective-permute-start.2 = (f32[3,6,16,128]{3,2,1,0:T(8,128)S(1)}, f32[3,6,16,128]{3,2,1,0:T(8,128)S(1)}, u32[]{:S(2)}, u32[]{:S(2)}) collective-permute-start(f32[3,6,16,128]{3,2,1,0:T(8,128)S(1)} %get-tuple-element.5), channel_id=1, source_target_pairs={{32,0},{64,32},{96,64},{128,96},{160,128},{192,160},{224,192},{256... | collective-permute-start | bytes 442376 | tf_op jit(solution)/shard_map/ppermute | solution.py:33
  86.4 2.9 collective-permute-done.2
  92.7 6.0 %collective-permute-start.4 = (f32[3,6,16,128]{3,2,1,0:T(8,128)S(1)}, f32[3,6,16,128]{3,2,1,0:T(8,128)S(1)}, u32[]{:S(2)}, u32[]{:S(2)}) collective-permute-start(f32[3,6,16,128]{3,2,1,0:T(8,128)S(1)} %fusion.260), channel_id=1, source_target_pairs={{32,0},{64,32},{96,64},{128,96},{160,128},{192,160},{224,192},{256... | collective-permute-start | bytes 442376 | tf_op jit(solution)/shard_map/ppermute | solution.py:33
  100.4 2.9 collective-permute-done.4
  105.8 6.0 %collective-permute-start.6 = (f32[3,6,16,128]{3,2,1,0:T(8,128)S(1)}, f32[3,6,16,128]{3,2,1,0:T(8,128)S(1)}, u32[]{:S(2)}, u32[]{:S(2)}) collective-permute-start(f32[3,6,16,128]{3,2,1,0:T(8,128)S(1)} %fusion.225), channel_id=1, source_target_pairs={{32,0},{64,32},{96,64},{128,96},{160,128},{192,160},{224,192},{256... | collective-permute-start | bytes 442376 | tf_op jit(solution)/shard_map/ppermute | solution.py:33
  113.5 2.9 collective-permute-done.6
  118.9 6.0 %collective-permute-start.8 = (f32[3,6,16,128]{3,2,1,0:T(8,128)S(1)}, f32[3,6,16,128]{3,2,1,0:T(8,128)S(1)}, u32[]{:S(2)}, u32[]{:S(2)}) collective-permute-start(f32[3,6,16,128]{3,2,1,0:T(8,128)S(1)} %fusion.190), channel_id=1, source_target_pairs={{32,0},{64,32},{96,64},{128,96},{160,128},{192,160},{224,192},{256... | collective-permute-start | bytes 442376 | tf_op jit(solution)/shard_map/ppermute | solution.py:33
  126.6 2.9 collective-permute-done.8
  131.9 6.0 %collective-permute-start.10 = (f32[3,6,16,128]{3,2,1,0:T(8,128)S(1)}, f32[3,6,16,128]{3,2,1,0:T(8,128)S(1)}, u32[]{:S(2)}, u32[]{:S(2)}) collective-permute-start(f32[3,6,16,128]{3,2,1,0:T(8,128)S(1)} %fusion.155), channel_id=1, source_target_pairs={{32,0},{64,32},{96,64},{128,96},{160,128},{192,160},{224,192},{256... | collective-permute-start | bytes 442376 | tf_op jit(solution)/shard_map/ppermute | solution.py:33
  139.7 2.9 collective-permute-done.10
  145.0 6.0 %collective-permute-start.12 = (f32[3,6,16,128]{3,2,1,0:T(8,128)S(1)}, f32[3,6,16,128]{3,2,1,0:T(8,128)S(1)}, u32[]{:S(2)}, u32[]{:S(2)}) collective-permute-start(f32[3,6,16,128]{3,2,1,0:T(8,128)S(1)} %fusion.120), channel_id=1, source_target_pairs={{32,0},{64,32},{96,64},{128,96},{160,128},{192,160},{224,192},{256... | collective-permute-start | bytes 442376 | tf_op jit(solution)/shard_map/ppermute | solution.py:33
  152.8 2.9 collective-permute-done.12
  158.1 6.0 %collective-permute-start.14 = (f32[3,6,16,128]{3,2,1,0:T(8,128)S(1)}, f32[3,6,16,128]{3,2,1,0:T(8,128)S(1)}, u32[]{:S(2)}, u32[]{:S(2)}) collective-permute-start(f32[3,6,16,128]{3,2,1,0:T(8,128)S(1)} %fusion.85), channel_id=1, source_target_pairs={{32,0},{64,32},{96,64},{128,96},{160,128},{192,160},{224,192},{256... | collective-permute-start | bytes 442376 | tf_op jit(solution)/shard_map/ppermute | solution.py:33
  165.9 2.9 collective-permute-done.14
  172.0 6.2 %collective-permute-start.16 = (f32[3,6,16,128]{3,2,1,0:T(8,128)S(1)}, f32[3,6,16,128]{3,2,1,0:T(8,128)S(1)}, u32[]{:S(2)}, u32[]{:S(2)}) collective-permute-start(f32[3,6,16,128]{3,2,1,0:T(8,128)S(1)} %fusion.50), channel_id=1, source_target_pairs={{32,0},{64,32},{96,64},{128,96},{160,128},{192,160},{224,192},{256... | collective-permute-start | bytes 442376 | tf_op jit(solution)/shard_map/ppermute | solution.py:33
  183.2 90.4 %all-gather.3.cloned.1.call-done = f32[32,3,12288]{2,1,0:T(4,128)} async-done(((f32[1,3,12288]{2,1,0:T(4,128)}), f32[32,3,12288]{2,1,0:T(4,128)}) %all-gather.3.cloned.1.call-update) | async-done | bytes 4718608 | tf_op jit(solution)/shard_map/all_gather | solution.py:123
  273.6 6.5 %reshape.16 = f32[96,12288]{1,0:T(8,128)} reshape(f32[32,3,12288]{2,1,0:T(4,128)} %all-gather.3.cloned.1.call-done) | data formatting | bytes 9437184
  280.1 5.7 %fusion.3 = f32[3,96]{1,0:T(4,128)S(1)} fusion(f32[96,12288]{1,0:T(8,128)} %reshape.16, f32[1,3,96,128]{3,2,1,0:T(8,128)S(1)} %bitcast.14), kind=kOutput, calls=%fused_computation.347 | convolution fusion | flops 42467328 | bytes 4867200 | tf_op jit(solution)/shard_map/dot_general | solution.py:91
  285.7 3.8 %fusion = f32[3,96]{1,0:T(4,128)S(1)} fusion(f32[96,12288]{1,0:T(8,128)S(1)} %copy-done, f32[1,3,96,128]{3,2,1,0:T(8,128)S(1)} %bitcast.15), kind=kOutput, calls=%fused_computation.344 | convolution fusion | flops 42467328 | bytes 4867200 | tf_op jit(solution)/shard_map/dot_general | solution.py:91
  289.5 65.4 %all-reduce.9 = (f32[3,96]{1,0:T(4,128)S(1)}, f32[3,96]{1,0:T(4,128)S(1)}) all-reduce(f32[3,96]{1,0:T(4,128)S(1)} %fusion.3, f32[3,96]{1,0:T(4,128)S(1)} %fusion), channel_id=1, replica_groups=mesh['domain'=32,'band'=32] {'domain'}, use_global_device_ids=true, to_apply=%region_0.1 | all-reduce | flops 576 | bytes 4608 | tf_op jit(solution)/shard_map/psum | solution.py:126
  (41 shorter events, 40.8 us)
Async XLA Ops:
  7.2 266.4 %all-gather.3.cloned.1.call-start = ((), (), s32[]{:S(2)}) async-start(), calls=%async_computation | async-start | bytes 6488064 | tf_op jit(solution)/shard_map/all_gather | solution.py:123
  7.2 63.1 %collective-permute-start.1 = (f32[3,6,16,128]{3,2,1,0:T(8,128)}, f32[3,6,16,128]{3,2,1,0:T(8,128)S(1)}, u32[]{:S(2)}, u32[]{:S(2)}) collective-permute-start(f32[3,6,16,128]{3,2,1,0:T(8,128)} %param.2), channel_id=1, source_target_pairs={{0,32},{32,64},{64,96},{96,128},{128,160},{160,192},{192,224},{224... | collective-permute-start | bytes 442376 | tf_op jit(solution)/shard_map/ppermute | solution.py:31
  10.6 60.7 %collective-permute-start = (f32[3,6,16,128]{3,2,1,0:T(8,128)}, f32[3,6,16,128]{3,2,1,0:T(8,128)S(1)}, u32[]{:S(2)}, u32[]{:S(2)}) collective-permute-start(f32[3,6,16,128]{3,2,1,0:T(8,128)} %param.2), channel_id=1, source_target_pairs={{32,0},{64,32},{96,64},{128,96},{160,128},{192,160},{224,192},{256... | collective-permute-start | bytes 442376 | tf_op jit(solution)/shard_map/ppermute | solution.py:33
  76.2 10.2 %collective-permute-start.3 = (f32[3,6,16,128]{3,2,1,0:T(8,128)S(1)}, f32[3,6,16,128]{3,2,1,0:T(8,128)S(1)}, u32[]{:S(2)}, u32[]{:S(2)}) collective-permute-start(f32[3,6,16,128]{3,2,1,0:T(8,128)S(1)} %get-tuple-element.5), channel_id=1, source_target_pairs={{0,32},{32,64},{64,96},{96,128},{128,160},{160,192},{192,224},{224... | collective-permute-start | bytes 442376 | tf_op jit(solution)/shard_map/ppermute | solution.py:31
  78.1 11.2 %collective-permute-start.2 = (f32[3,6,16,128]{3,2,1,0:T(8,128)S(1)}, f32[3,6,16,128]{3,2,1,0:T(8,128)S(1)}, u32[]{:S(2)}, u32[]{:S(2)}) collective-permute-start(f32[3,6,16,128]{3,2,1,0:T(8,128)S(1)} %get-tuple-element.5), channel_id=1, source_target_pairs={{32,0},{64,32},{96,64},{128,96},{160,128},{192,160},{224,192},{256... | collective-permute-start | bytes 442376 | tf_op jit(solution)/shard_map/ppermute | solution.py:33
  90.7 9.7 %collective-permute-start.5 = (f32[3,6,16,128]{3,2,1,0:T(8,128)S(1)}, f32[3,6,16,128]{3,2,1,0:T(8,128)S(1)}, u32[]{:S(2)}, u32[]{:S(2)}) collective-permute-start(f32[3,6,16,128]{3,2,1,0:T(8,128)S(1)} %fusion.260), channel_id=1, source_target_pairs={{0,32},{32,64},{64,96},{96,128},{128,160},{160,192},{192,224},{224... | collective-permute-start | bytes 442376 | tf_op jit(solution)/shard_map/ppermute | solution.py:31
  92.7 10.6 %collective-permute-start.4 = (f32[3,6,16,128]{3,2,1,0:T(8,128)S(1)}, f32[3,6,16,128]{3,2,1,0:T(8,128)S(1)}, u32[]{:S(2)}, u32[]{:S(2)}) collective-permute-start(f32[3,6,16,128]{3,2,1,0:T(8,128)S(1)} %fusion.260), channel_id=1, source_target_pairs={{32,0},{64,32},{96,64},{128,96},{160,128},{192,160},{224,192},{256... | collective-permute-start | bytes 442376 | tf_op jit(solution)/shard_map/ppermute | solution.py:33
  103.8 9.7 %collective-permute-start.7 = (f32[3,6,16,128]{3,2,1,0:T(8,128)S(1)}, f32[3,6,16,128]{3,2,1,0:T(8,128)S(1)}, u32[]{:S(2)}, u32[]{:S(2)}) collective-permute-start(f32[3,6,16,128]{3,2,1,0:T(8,128)S(1)} %fusion.225), channel_id=1, source_target_pairs={{0,32},{32,64},{64,96},{96,128},{128,160},{160,192},{192,224},{224... | collective-permute-start | bytes 442376 | tf_op jit(solution)/shard_map/ppermute | solution.py:31
  105.8 10.6 %collective-permute-start.6 = (f32[3,6,16,128]{3,2,1,0:T(8,128)S(1)}, f32[3,6,16,128]{3,2,1,0:T(8,128)S(1)}, u32[]{:S(2)}, u32[]{:S(2)}) collective-permute-start(f32[3,6,16,128]{3,2,1,0:T(8,128)S(1)} %fusion.225), channel_id=1, source_target_pairs={{32,0},{64,32},{96,64},{128,96},{160,128},{192,160},{224,192},{256... | collective-permute-start | bytes 442376 | tf_op jit(solution)/shard_map/ppermute | solution.py:33
  116.9 9.7 %collective-permute-start.9 = (f32[3,6,16,128]{3,2,1,0:T(8,128)S(1)}, f32[3,6,16,128]{3,2,1,0:T(8,128)S(1)}, u32[]{:S(2)}, u32[]{:S(2)}) collective-permute-start(f32[3,6,16,128]{3,2,1,0:T(8,128)S(1)} %fusion.190), channel_id=1, source_target_pairs={{0,32},{32,64},{64,96},{96,128},{128,160},{160,192},{192,224},{224... | collective-permute-start | bytes 442376 | tf_op jit(solution)/shard_map/ppermute | solution.py:31
  118.9 10.6 %collective-permute-start.8 = (f32[3,6,16,128]{3,2,1,0:T(8,128)S(1)}, f32[3,6,16,128]{3,2,1,0:T(8,128)S(1)}, u32[]{:S(2)}, u32[]{:S(2)}) collective-permute-start(f32[3,6,16,128]{3,2,1,0:T(8,128)S(1)} %fusion.190), channel_id=1, source_target_pairs={{32,0},{64,32},{96,64},{128,96},{160,128},{192,160},{224,192},{256... | collective-permute-start | bytes 442376 | tf_op jit(solution)/shard_map/ppermute | solution.py:33
  130.0 9.7 %collective-permute-start.11 = (f32[3,6,16,128]{3,2,1,0:T(8,128)S(1)}, f32[3,6,16,128]{3,2,1,0:T(8,128)S(1)}, u32[]{:S(2)}, u32[]{:S(2)}) collective-permute-start(f32[3,6,16,128]{3,2,1,0:T(8,128)S(1)} %fusion.155), channel_id=1, source_target_pairs={{0,32},{32,64},{64,96},{96,128},{128,160},{160,192},{192,224},{224... | collective-permute-start | bytes 442376 | tf_op jit(solution)/shard_map/ppermute | solution.py:31
  131.9 10.6 %collective-permute-start.10 = (f32[3,6,16,128]{3,2,1,0:T(8,128)S(1)}, f32[3,6,16,128]{3,2,1,0:T(8,128)S(1)}, u32[]{:S(2)}, u32[]{:S(2)}) collective-permute-start(f32[3,6,16,128]{3,2,1,0:T(8,128)S(1)} %fusion.155), channel_id=1, source_target_pairs={{32,0},{64,32},{96,64},{128,96},{160,128},{192,160},{224,192},{256... | collective-permute-start | bytes 442376 | tf_op jit(solution)/shard_map/ppermute | solution.py:33
  143.1 9.7 %collective-permute-start.13 = (f32[3,6,16,128]{3,2,1,0:T(8,128)S(1)}, f32[3,6,16,128]{3,2,1,0:T(8,128)S(1)}, u32[]{:S(2)}, u32[]{:S(2)}) collective-permute-start(f32[3,6,16,128]{3,2,1,0:T(8,128)S(1)} %fusion.120), channel_id=1, source_target_pairs={{0,32},{32,64},{64,96},{96,128},{128,160},{160,192},{192,224},{224... | collective-permute-start | bytes 442376 | tf_op jit(solution)/shard_map/ppermute | solution.py:31
  145.0 10.6 %collective-permute-start.12 = (f32[3,6,16,128]{3,2,1,0:T(8,128)S(1)}, f32[3,6,16,128]{3,2,1,0:T(8,128)S(1)}, u32[]{:S(2)}, u32[]{:S(2)}) collective-permute-start(f32[3,6,16,128]{3,2,1,0:T(8,128)S(1)} %fusion.120), channel_id=1, source_target_pairs={{32,0},{64,32},{96,64},{128,96},{160,128},{192,160},{224,192},{256... | collective-permute-start | bytes 442376 | tf_op jit(solution)/shard_map/ppermute | solution.py:33
  156.2 9.7 %collective-permute-start.15 = (f32[3,6,16,128]{3,2,1,0:T(8,128)S(1)}, f32[3,6,16,128]{3,2,1,0:T(8,128)S(1)}, u32[]{:S(2)}, u32[]{:S(2)}) collective-permute-start(f32[3,6,16,128]{3,2,1,0:T(8,128)S(1)} %fusion.85), channel_id=1, source_target_pairs={{0,32},{32,64},{64,96},{96,128},{128,160},{160,192},{192,224},{224... | collective-permute-start | bytes 442376 | tf_op jit(solution)/shard_map/ppermute | solution.py:31
  158.1 10.6 %collective-permute-start.14 = (f32[3,6,16,128]{3,2,1,0:T(8,128)S(1)}, f32[3,6,16,128]{3,2,1,0:T(8,128)S(1)}, u32[]{:S(2)}, u32[]{:S(2)}) collective-permute-start(f32[3,6,16,128]{3,2,1,0:T(8,128)S(1)} %fusion.85), channel_id=1, source_target_pairs={{32,0},{64,32},{96,64},{128,96},{160,128},{192,160},{224,192},{256... | collective-permute-start | bytes 442376 | tf_op jit(solution)/shard_map/ppermute | solution.py:33
  169.3 110.7 %copy-start.1 = (f32[3,6,16,128]{3,2,1,0:T(8,128)}, f32[3,6,16,128]{3,2,1,0:T(8,128)S(1)}, u32[]{:S(2)}) copy-start(f32[3,6,16,128]{3,2,1,0:T(8,128)S(1)} %fusion.50) | copy-start | bytes 442372
  170.1 9.7 %collective-permute-start.17 = (f32[3,6,16,128]{3,2,1,0:T(8,128)S(1)}, f32[3,6,16,128]{3,2,1,0:T(8,128)S(1)}, u32[]{:S(2)}, u32[]{:S(2)}) collective-permute-start(f32[3,6,16,128]{3,2,1,0:T(8,128)S(1)} %fusion.50), channel_id=1, source_target_pairs={{0,32},{32,64},{64,96},{96,128},{128,160},{160,192},{192,224},{224... | collective-permute-start | bytes 442376 | tf_op jit(solution)/shard_map/ppermute | solution.py:31
  172.0 10.6 %collective-permute-start.16 = (f32[3,6,16,128]{3,2,1,0:T(8,128)S(1)}, f32[3,6,16,128]{3,2,1,0:T(8,128)S(1)}, u32[]{:S(2)}, u32[]{:S(2)}) collective-permute-start(f32[3,6,16,128]{3,2,1,0:T(8,128)S(1)} %fusion.50), channel_id=1, source_target_pairs={{32,0},{64,32},{96,64},{128,96},{160,128},{192,160},{224,192},{256... | collective-permute-start | bytes 442376 | tf_op jit(solution)/shard_map/ppermute | solution.py:33
  280.0 5.7 %copy-start = (f32[96,12288]{1,0:T(8,128)S(1)}, f32[96,12288]{1,0:T(8,128)}, u32[]{:S(2)}) copy-start(f32[96,12288]{1,0:T(8,128)} %reshape.16) | copy-start | bytes 14155780
Sparse Core Ops, SparseCore 0:
  170.2 103.3 all-gather.2
where the time goes:
time: 363 us; the launch traced here: 362 us
  waiting for transfers between devices  127 us (35%)
  blocking collectives  107 us (29%)
  starting transfers between devices  84.9 us (23%)
  between operations  14.2 us (4%)
  other arithmetic  10.6 us (3%)
  matrix products  9.46 us (3%)
  local copies, waits for them, and re-layouts  9.06 us (2%)
    all_gather x1, waiting for transfers between devices, body(): panel_in = lax.all_gather(flat_panel, 'band', axis=0, tiled=True)  90.4 us
    ppermute x9, starting transfers between devices, extended(): lax.ppermute(head, axis, [((i + 1) % count, i) for i in range(count)])  66.1 us
    psum x1, blocking collectives, body(): s_total, h_total = lax.psum((s_part, h_part), 'domain')  65.4 us
    all_gather x1, blocking collectives, body(): local_pot = lax.all_gather(potential, 'band', axis=2, tiled=True)  41.2 us
    ppermute x9, waiting for transfers between devices, extended(): lax.ppermute(head, axis, [((i + 1) % count, i) for i in range(count)])  23 us
    ppermute x9, starting transfers between devices, extended(): lax.ppermute(tail, axis, [(i, (i + 1) % count) for i in range(count)])  18.8 us
    ppermute x9, waiting for transfers between devices, extended(): lax.ppermute(tail, axis, [(i, (i + 1) % count) for i in range(count)])  14.2 us
    dot_general x2, matrix products, contract(): lax.dot_general(left, right, (((1,), (1,)), ((), ())), precision=lax.Prec...  9.46 us
  transfers between devices with their start and end apart: 19, of which 17 were waited for; matrix products, arithmetic and copies ran while one was open for 1% of the time, Pallas kernels for 0%

commit v1 on v0

--- a/solution.py
+++ b/solution.py
@@ -97,8 +97,36 @@
     )
 
 
+def gather_potential(potential):
+    parts = lax.axis_size("band")
+    sent = jnp.broadcast_to(potential[None], (parts,) + potential.shape)
+    got = lax.all_to_all(sent, "band", 0, 0, tiled=True)
+    planes, size_y, slab = potential.shape
+    return got.transpose(1, 2, 0, 3).reshape(planes, size_y, parts * slab)
+
+
+def gram_rows(flat_panel, flat_image):
+    parts = lax.axis_size("band")
+    orb_dev, cells = flat_panel.shape
+    share = cells // parts
+    both = jnp.concatenate([flat_panel, flat_image], axis=0)
+    both = both.reshape(2 * orb_dev, parts, share).transpose(1, 0, 2)
+    got = lax.all_to_all(both, "band", 0, 0, tiled=True)
+    panel_all = got[:, :orb_dev].reshape(parts * orb_dev, share)
+    image_all = got[:, orb_dev:].reshape(parts * orb_dev, share)
+    s_part = contract(panel_all, panel_all)
+    h_part = contract(image_all, panel_all)
+    tiles = jnp.stack([s_part, h_part]).reshape(2, parts, orb_dev, parts * orb_dev)
+    got = lax.all_to_all(tiles.transpose(1, 0, 2, 3), "band", 0, 0, tiled=True)
+    rows = jnp.sum(got, axis=0)
+    count = lax.axis_size("domain")
+    sent = jnp.broadcast_to(rows[None], (count,) + rows.shape)
+    got = lax.all_to_all(sent, "domain", 0, 0, tiled=True)
+    return jnp.sum(got, axis=0)
+
+
 def body(orbitals, potential):
-    local_pot = lax.all_gather(potential, "band", axis=2, tiled=True)
+    local_pot = gather_potential(potential)
     half_width = (upper_bound - lower_bound) / 2.0
     centre = (upper_bound + lower_bound) / 2.0
     sigma_first = half_width / (lowest_bound - centre)
@@ -118,14 +146,9 @@
     h_image = apply_hamiltonian(current, local_pot)
     orb_dev = current.shape[0]
     cell_count = current.shape[1] * current.shape[2] * current.shape[3] * lax.axis_size("domain")
-    flat_panel = current.reshape(orb_dev, -1)
-    flat_image = h_image.reshape(orb_dev, -1)
-    panel_in = lax.all_gather(flat_panel, "band", axis=0, tiled=True)
-    s_part = contract(flat_panel, panel_in)
-    h_part = contract(flat_image, panel_in)
-    s_total, h_total = lax.psum((s_part, h_part), "domain")
-    intersection = s_total / cell_count
-    hamiltonian = h_total / cell_count
+    totals = gram_rows(current.reshape(orb_dev, -1), h_image.reshape(orb_dev, -1))
+    intersection = totals[0] / cell_count
+    hamiltonian = totals[1] / cell_count
     return (current, intersection, hamiltonian)
 
 

time: 363 us -> 208 us (0.57)
  the two profiles are of different devices: /device:TPU:8 before, /device:TPU:2 now
where the time goes in v1:
time: 208 us; the launch traced here: 207 us
  starting transfers between devices  85 us (41%)
  blocking collectives  62.7 us (30%)
  waiting for transfers between devices  47.6 us (23%)
  other arithmetic  5.79 us (3%)
  local copies, waits for them, and re-layouts  4.03 us (2%)
    ppermute x9, starting transfers between devices, extended(): lax.ppermute(head, axis, [((i + 1) % count, i) for i in range(count)])  55.5 us
    ppermute x9, waiting for transfers between devices, extended(): lax.ppermute(tail, axis, [(i, (i + 1) % count) for i in range(count)])  41.9 us
    all_to_all x1, blocking collectives, gram_rows(): got = lax.all_to_all(both, 'band', 0, 0, tiled=True)  24.1 us
    all_to_all x1, blocking collectives, gram_rows(): got = lax.all_to_all(sent, 'domain', 0, 0, tiled=True)  24 us
    ppermute x9, starting transfers between devices, extended(): lax.ppermute(tail, axis, [(i, (i + 1) % count) for i in range(count)])  20.5 us
    all_to_all x1, blocking collectives, gram_rows(): got = lax.all_to_all(tiles.transpose(1, 0, 2, 3), 'band', 0, 0, tiled=True)  14.6 us
    all_to_all x1, starting transfers between devices, gather_potential(): got = lax.all_to_all(sent, 'band', 0, 0, tiled=True)  9.05 us
    ppermute x9, waiting for transfers between devices, extended(): lax.ppermute(head, axis, [((i + 1) % count, i) for i in range(count)])  5.65 us
  transfers between devices with their start and end apart: 19, of which 17 were waited for; matrix products, arithmetic and copies ran while one was open for 1% of the time, Pallas kernels for 0%

profile of v1, /device:TPU:2, one launch (start us, length us, event | category | flops | bytes accessed | tf_op | source)
XLA Modules:
  0.0 206.8 jit_solution(8823067376679132516)
XLA Ops:
  2.4 9.1 %all-to-all-start = ((f32[32,1,384]{2,1,0:T(1,128)}), f32[32,1,384]{2,1,0:T(1,128)S(1)}, u32[]{:S(2)}, u32[]{:S(2)}) async-start(f32[32,1,384]{2,1,0:T(1,128)} %reshape.42), calls=%async_computation | async-start | bytes 98304 | tf_op jit(solution)/shard_map/all_to_all | solution.py:103
  11.4 5.2 %collective-permute-start.1 = (f32[3,6,16,128]{3,2,1,0:T(8,128)S(1)}, f32[3,6,16,128]{3,2,1,0:T(8,128)S(1)}, u32[]{:S(2)}, u32[]{:S(2)}) collective-permute-start(f32[3,6,16,128]{3,2,1,0:T(8,128)S(1)} %copy-done.1), channel_id=1, source_target_pairs={{0,32},{32,64},{64,96},{96,128},{128,160},{160,192},{192,224},{224... | collective-permute-start | bytes 442376 | tf_op jit(solution)/shard_map/ppermute | solution.py:31
  16.6 6.7 %collective-permute-start = (f32[3,6,16,128]{3,2,1,0:T(8,128)S(1)}, f32[3,6,16,128]{3,2,1,0:T(8,128)S(1)}, u32[]{:S(2)}, u32[]{:S(2)}) collective-permute-start(f32[3,6,16,128]{3,2,1,0:T(8,128)S(1)} %copy-done.1), channel_id=1, source_target_pairs={{32,0},{64,32},{96,64},{128,96},{160,128},{192,160},{224,192},{256... | collective-permute-start | bytes 442376 | tf_op jit(solution)/shard_map/ppermute | solution.py:33
  25.1 3.6 %collective-permute-done.1 = f32[3,6,16,128]{3,2,1,0:T(8,128)S(1)} collective-permute-done((f32[3,6,16,128]{3,2,1,0:T(8,128)S(1)}, f32[3,6,16,128]{3,2,1,0:T(8,128)S(1)}, u32[]{:S(2)}, u32[]{:S(2)}) %collective-permute-start.1) | collective-permute-done | bytes 147488 | tf_op jit(solution)/shard_map/ppermute | solution.py:31
  29.3 9.7 %collective-permute-start.2 = (f32[3,6,16,128]{3,2,1,0:T(8,128)S(1)}, f32[3,6,16,128]{3,2,1,0:T(8,128)S(1)}, u32[]{:S(2)}, u32[]{:S(2)}) collective-permute-start(f32[3,6,16,128]{3,2,1,0:T(8,128)S(1)} %get-tuple-element.3), channel_id=1, source_target_pairs={{32,0},{64,32},{96,64},{128,96},{160,128},{192,160},{224,192},{256... | collective-permute-start | bytes 442376 | tf_op jit(solution)/shard_map/ppermute | solution.py:33
  41.8 7.5 %collective-permute-done.3 = f32[3,6,16,128]{3,2,1,0:T(8,128)S(1)} collective-permute-done((f32[3,6,16,128]{3,2,1,0:T(8,128)S(1)}, f32[3,6,16,128]{3,2,1,0:T(8,128)S(1)}, u32[]{:S(2)}, u32[]{:S(2)}) %collective-permute-start.3) | collective-permute-done | bytes 147488 | tf_op jit(solution)/shard_map/ppermute | solution.py:31
  49.8 5.8 %collective-permute-start.4 = (f32[3,6,16,128]{3,2,1,0:T(8,128)S(1)}, f32[3,6,16,128]{3,2,1,0:T(8,128)S(1)}, u32[]{:S(2)}, u32[]{:S(2)}) collective-permute-start(f32[3,6,16,128]{3,2,1,0:T(8,128)S(1)} %fusion.254), channel_id=1, source_target_pairs={{32,0},{64,32},{96,64},{128,96},{160,128},{192,160},{224,192},{256... | collective-permute-start | bytes 442376 | tf_op jit(solution)/shard_map/ppermute | solution.py:33
  58.2 4.5 %collective-permute-done.5 = f32[3,6,16,128]{3,2,1,0:T(8,128)S(1)} collective-permute-done((f32[3,6,16,128]{3,2,1,0:T(8,128)S(1)}, f32[3,6,16,128]{3,2,1,0:T(8,128)S(1)}, u32[]{:S(2)}, u32[]{:S(2)}) %collective-permute-start.5) | collective-permute-done | bytes 147488 | tf_op jit(solution)/shard_map/ppermute | solution.py:31
  63.2 5.8 %collective-permute-start.6 = (f32[3,6,16,128]{3,2,1,0:T(8,128)S(1)}, f32[3,6,16,128]{3,2,1,0:T(8,128)S(1)}, u32[]{:S(2)}, u32[]{:S(2)}) collective-permute-start(f32[3,6,16,128]{3,2,1,0:T(8,128)S(1)} %fusion.219), channel_id=1, source_target_pairs={{32,0},{64,32},{96,64},{128,96},{160,128},{192,160},{224,192},{256... | collective-permute-start | bytes 442376 | tf_op jit(solution)/shard_map/ppermute | solution.py:33
  69.0 1.9 collective-permute-start.7
  71.7 4.4 %collective-permute-done.7 = f32[3,6,16,128]{3,2,1,0:T(8,128)S(1)} collective-permute-done((f32[3,6,16,128]{3,2,1,0:T(8,128)S(1)}, f32[3,6,16,128]{3,2,1,0:T(8,128)S(1)}, u32[]{:S(2)}, u32[]{:S(2)}) %collective-permute-start.7) | collective-permute-done | bytes 147488 | tf_op jit(solution)/shard_map/ppermute | solution.py:31
  76.6 5.5 %collective-permute-start.8 = (f32[3,6,16,128]{3,2,1,0:T(8,128)S(1)}, f32[3,6,16,128]{3,2,1,0:T(8,128)S(1)}, u32[]{:S(2)}, u32[]{:S(2)}) collective-permute-start(f32[3,6,16,128]{3,2,1,0:T(8,128)S(1)} %fusion.184), channel_id=1, source_target_pairs={{32,0},{64,32},{96,64},{128,96},{160,128},{192,160},{224,192},{256... | collective-permute-start | bytes 442376 | tf_op jit(solution)/shard_map/ppermute | solution.py:33
  84.8 4.4 %collective-permute-done.9 = f32[3,6,16,128]{3,2,1,0:T(8,128)S(1)} collective-permute-done((f32[3,6,16,128]{3,2,1,0:T(8,128)S(1)}, f32[3,6,16,128]{3,2,1,0:T(8,128)S(1)}, u32[]{:S(2)}, u32[]{:S(2)}) %collective-permute-start.9) | collective-permute-done | bytes 147488 | tf_op jit(solution)/shard_map/ppermute | solution.py:31
  89.7 5.5 %collective-permute-start.10 = (f32[3,6,16,128]{3,2,1,0:T(8,128)S(1)}, f32[3,6,16,128]{3,2,1,0:T(8,128)S(1)}, u32[]{:S(2)}, u32[]{:S(2)}) collective-permute-start(f32[3,6,16,128]{3,2,1,0:T(8,128)S(1)} %fusion.149), channel_id=1, source_target_pairs={{32,0},{64,32},{96,64},{128,96},{160,128},{192,160},{224,192},{256... | collective-permute-start | bytes 442376 | tf_op jit(solution)/shard_map/ppermute | solution.py:33
  97.9 4.4 %collective-permute-done.11 = f32[3,6,16,128]{3,2,1,0:T(8,128)S(1)} collective-permute-done((f32[3,6,16,128]{3,2,1,0:T(8,128)S(1)}, f32[3,6,16,128]{3,2,1,0:T(8,128)S(1)}, u32[]{:S(2)}, u32[]{:S(2)}) %collective-permute-start.11) | collective-permute-done | bytes 147488 | tf_op jit(solution)/shard_map/ppermute | solution.py:31
  102.8 5.5 %collective-permute-start.12 = (f32[3,6,16,128]{3,2,1,0:T(8,128)S(1)}, f32[3,6,16,128]{3,2,1,0:T(8,128)S(1)}, u32[]{:S(2)}, u32[]{:S(2)}) collective-permute-start(f32[3,6,16,128]{3,2,1,0:T(8,128)S(1)} %fusion.114), channel_id=1, source_target_pairs={{32,0},{64,32},{96,64},{128,96},{160,128},{192,160},{224,192},{256... | collective-permute-start | bytes 442376 | tf_op jit(solution)/shard_map/ppermute | solution.py:33
  111.0 4.4 %collective-permute-done.13 = f32[3,6,16,128]{3,2,1,0:T(8,128)S(1)} collective-permute-done((f32[3,6,16,128]{3,2,1,0:T(8,128)S(1)}, f32[3,6,16,128]{3,2,1,0:T(8,128)S(1)}, u32[]{:S(2)}, u32[]{:S(2)}) %collective-permute-start.13) | collective-permute-done | bytes 147488 | tf_op jit(solution)/shard_map/ppermute | solution.py:31
  115.9 5.5 %collective-permute-start.14 = (f32[3,6,16,128]{3,2,1,0:T(8,128)S(1)}, f32[3,6,16,128]{3,2,1,0:T(8,128)S(1)}, u32[]{:S(2)}, u32[]{:S(2)}) collective-permute-start(f32[3,6,16,128]{3,2,1,0:T(8,128)S(1)} %fusion.79), channel_id=1, source_target_pairs={{32,0},{64,32},{96,64},{128,96},{160,128},{192,160},{224,192},{256... | collective-permute-start | bytes 442376 | tf_op jit(solution)/shard_map/ppermute | solution.py:33
  124.1 4.4 %collective-permute-done.15 = f32[3,6,16,128]{3,2,1,0:T(8,128)S(1)} collective-permute-done((f32[3,6,16,128]{3,2,1,0:T(8,128)S(1)}, f32[3,6,16,128]{3,2,1,0:T(8,128)S(1)}, u32[]{:S(2)}, u32[]{:S(2)}) %collective-permute-start.15) | collective-permute-done | bytes 147488 | tf_op jit(solution)/shard_map/ppermute | solution.py:31
  129.0 5.5 %collective-permute-start.16 = (f32[3,6,16,128]{3,2,1,0:T(8,128)S(1)}, f32[3,6,16,128]{3,2,1,0:T(8,128)S(1)}, u32[]{:S(2)}, u32[]{:S(2)}) collective-permute-start(f32[3,6,16,128]{3,2,1,0:T(8,128)S(1)} %fusion.44), channel_id=1, source_target_pairs={{32,0},{64,32},{96,64},{128,96},{160,128},{192,160},{224,192},{256... | collective-permute-start | bytes 442376 | tf_op jit(solution)/shard_map/ppermute | solution.py:33
  137.2 4.4 %collective-permute-done.17 = f32[3,6,16,128]{3,2,1,0:T(8,128)S(1)} collective-permute-done((f32[3,6,16,128]{3,2,1,0:T(8,128)S(1)}, f32[3,6,16,128]{3,2,1,0:T(8,128)S(1)}, u32[]{:S(2)}, u32[]{:S(2)}) %collective-permute-start.17) | collective-permute-done | bytes 147488 | tf_op jit(solution)/shard_map/ppermute | solution.py:31
  142.4 24.1 %all_to_all.20 = f32[32,6,384]{2,1,0:T(8,128)S(1)} all-to-all(f32[32,6,384]{2,1,0:T(8,128)S(1)} %copy.28), channel_id=1, replica_groups=mesh['domain'=32,'band'=32] {'band'}, dimensions={0} | all-to-all | bytes 589824 | tf_op jit(solution)/shard_map/all_to_all | solution.py:114
  167.4 14.6 %all_to_all.21 = f32[32,2,3,96]{3,1,2,0:T(2,128)S(1)} all-to-all(f32[32,2,3,96]{3,1,2,0:T(2,128)S(1)} %copy.32), channel_id=1, replica_groups=mesh['domain'=32,'band'=32] {'band'}, dimensions={0} | all-to-all | bytes 147456 | tf_op jit(solution)/shard_map/all_to_all | solution.py:120
  182.1 24.0 %all_to_all.22 = f32[32,2,3,96]{3,1,2,0:T(2,128)S(1)} all-to-all(f32[32,2,3,96]{3,1,2,0:T(2,128)S(1)} %broadcast_in_dim.5), channel_id=1, replica_groups=mesh['domain'=32,'band'=32] {'domain'}, dimensions={0} | all-to-all | bytes 147456 | tf_op jit(solution)/shard_map/all_to_all | solution.py:124
  (60 shorter events, 29.5 us)
Async XLA Ops:
  0.6 0.7 copy-start
  1.4 10.0 %copy-start.1 = (f32[3,6,16,128]{3,2,1,0:T(8,128)S(1)}, f32[3,6,16,128]{3,2,1,0:T(8,128)}, u32[]{:S(2)}) copy-start(f32[3,6,16,128]{3,2,1,0:T(8,128)} %param.2) | copy-start | bytes 442372
  2.4 20.9 %all-to-all-start = ((f32[32,1,384]{2,1,0:T(1,128)}), f32[32,1,384]{2,1,0:T(1,128)S(1)}, u32[]{:S(2)}, u32[]{:S(2)}) async-start(f32[32,1,384]{2,1,0:T(1,128)} %reshape.42), calls=%async_computation | async-start | bytes 98304 | tf_op jit(solution)/shard_map/all_to_all | solution.py:103
  11.4 17.3 %collective-permute-start.1 = (f32[3,6,16,128]{3,2,1,0:T(8,128)S(1)}, f32[3,6,16,128]{3,2,1,0:T(8,128)S(1)}, u32[]{:S(2)}, u32[]{:S(2)}) collective-permute-start(f32[3,6,16,128]{3,2,1,0:T(8,128)S(1)} %copy-done.1), channel_id=1, source_target_pairs={{0,32},{32,64},{64,96},{96,128},{128,160},{160,192},{192,224},{224... | collective-permute-start | bytes 442376 | tf_op jit(solution)/shard_map/ppermute | solution.py:31
  16.6 12.2 %collective-permute-start = (f32[3,6,16,128]{3,2,1,0:T(8,128)S(1)}, f32[3,6,16,128]{3,2,1,0:T(8,128)S(1)}, u32[]{:S(2)}, u32[]{:S(2)}) collective-permute-start(f32[3,6,16,128]{3,2,1,0:T(8,128)S(1)} %copy-done.1), channel_id=1, source_target_pairs={{32,0},{64,32},{96,64},{128,96},{160,128},{192,160},{224,192},{256... | collective-permute-start | bytes 442376 | tf_op jit(solution)/shard_map/ppermute | solution.py:33
  29.3 12.4 %collective-permute-start.2 = (f32[3,6,16,128]{3,2,1,0:T(8,128)S(1)}, f32[3,6,16,128]{3,2,1,0:T(8,128)S(1)}, u32[]{:S(2)}, u32[]{:S(2)}) collective-permute-start(f32[3,6,16,128]{3,2,1,0:T(8,128)S(1)} %get-tuple-element.3), channel_id=1, source_target_pairs={{32,0},{64,32},{96,64},{128,96},{160,128},{192,160},{224,192},{256... | collective-permute-start | bytes 442376 | tf_op jit(solution)/shard_map/ppermute | solution.py:33
  39.1 10.2 %collective-permute-start.3 = (f32[3,6,16,128]{3,2,1,0:T(8,128)S(1)}, f32[3,6,16,128]{3,2,1,0:T(8,128)S(1)}, u32[]{:S(2)}, u32[]{:S(2)}) collective-permute-start(f32[3,6,16,128]{3,2,1,0:T(8,128)S(1)} %get-tuple-element.3), channel_id=1, source_target_pairs={{0,32},{32,64},{64,96},{96,128},{128,160},{160,192},{192,224},{224... | collective-permute-start | bytes 442376 | tf_op jit(solution)/shard_map/ppermute | solution.py:31
  49.8 8.4 %collective-permute-start.4 = (f32[3,6,16,128]{3,2,1,0:T(8,128)S(1)}, f32[3,6,16,128]{3,2,1,0:T(8,128)S(1)}, u32[]{:S(2)}, u32[]{:S(2)}) collective-permute-start(f32[3,6,16,128]{3,2,1,0:T(8,128)S(1)} %fusion.254), channel_id=1, source_target_pairs={{32,0},{64,32},{96,64},{128,96},{160,128},{192,160},{224,192},{256... | collective-permute-start | bytes 442376 | tf_op jit(solution)/shard_map/ppermute | solution.py:33
  55.5 7.2 %collective-permute-start.5 = (f32[3,6,16,128]{3,2,1,0:T(8,128)S(1)}, f32[3,6,16,128]{3,2,1,0:T(8,128)S(1)}, u32[]{:S(2)}, u32[]{:S(2)}) collective-permute-start(f32[3,6,16,128]{3,2,1,0:T(8,128)S(1)} %fusion.254), channel_id=1, source_target_pairs={{0,32},{32,64},{64,96},{96,128},{128,160},{160,192},{192,224},{224... | collective-permute-start | bytes 442376 | tf_op jit(solution)/shard_map/ppermute | solution.py:31
  63.2 8.4 %collective-permute-start.6 = (f32[3,6,16,128]{3,2,1,0:T(8,128)S(1)}, f32[3,6,16,128]{3,2,1,0:T(8,128)S(1)}, u32[]{:S(2)}, u32[]{:S(2)}) collective-permute-start(f32[3,6,16,128]{3,2,1,0:T(8,128)S(1)} %fusion.219), channel_id=1, source_target_pairs={{32,0},{64,32},{96,64},{128,96},{160,128},{192,160},{224,192},{256... | collective-permute-start | bytes 442376 | tf_op jit(solution)/shard_map/ppermute | solution.py:33
  69.0 7.0 %collective-permute-start.7 = (f32[3,6,16,128]{3,2,1,0:T(8,128)S(1)}, f32[3,6,16,128]{3,2,1,0:T(8,128)S(1)}, u32[]{:S(2)}, u32[]{:S(2)}) collective-permute-start(f32[3,6,16,128]{3,2,1,0:T(8,128)S(1)} %fusion.219), channel_id=1, source_target_pairs={{0,32},{32,64},{64,96},{96,128},{128,160},{160,192},{192,224},{224... | collective-permute-start | bytes 442376 | tf_op jit(solution)/shard_map/ppermute | solution.py:31
  76.6 8.2 %collective-permute-start.8 = (f32[3,6,16,128]{3,2,1,0:T(8,128)S(1)}, f32[3,6,16,128]{3,2,1,0:T(8,128)S(1)}, u32[]{:S(2)}, u32[]{:S(2)}) collective-permute-start(f32[3,6,16,128]{3,2,1,0:T(8,128)S(1)} %fusion.184), channel_id=1, source_target_pairs={{32,0},{64,32},{96,64},{128,96},{160,128},{192,160},{224,192},{256... | collective-permute-start | bytes 442376 | tf_op jit(solution)/shard_map/ppermute | solution.py:33
  82.1 7.0 %collective-permute-start.9 = (f32[3,6,16,128]{3,2,1,0:T(8,128)S(1)}, f32[3,6,16,128]{3,2,1,0:T(8,128)S(1)}, u32[]{:S(2)}, u32[]{:S(2)}) collective-permute-start(f32[3,6,16,128]{3,2,1,0:T(8,128)S(1)} %fusion.184), channel_id=1, source_target_pairs={{0,32},{32,64},{64,96},{96,128},{128,160},{160,192},{192,224},{224... | collective-permute-start | bytes 442376 | tf_op jit(solution)/shard_map/ppermute | solution.py:31
  89.7 8.2 %collective-permute-start.10 = (f32[3,6,16,128]{3,2,1,0:T(8,128)S(1)}, f32[3,6,16,128]{3,2,1,0:T(8,128)S(1)}, u32[]{:S(2)}, u32[]{:S(2)}) collective-permute-start(f32[3,6,16,128]{3,2,1,0:T(8,128)S(1)} %fusion.149), channel_id=1, source_target_pairs={{32,0},{64,32},{96,64},{128,96},{160,128},{192,160},{224,192},{256... | collective-permute-start | bytes 442376 | tf_op jit(solution)/shard_map/ppermute | solution.py:33
  95.2 7.0 %collective-permute-start.11 = (f32[3,6,16,128]{3,2,1,0:T(8,128)S(1)}, f32[3,6,16,128]{3,2,1,0:T(8,128)S(1)}, u32[]{:S(2)}, u32[]{:S(2)}) collective-permute-start(f32[3,6,16,128]{3,2,1,0:T(8,128)S(1)} %fusion.149), channel_id=1, source_target_pairs={{0,32},{32,64},{64,96},{96,128},{128,160},{160,192},{192,224},{224... | collective-permute-start | bytes 442376 | tf_op jit(solution)/shard_map/ppermute | solution.py:31
  102.8 8.2 %collective-permute-start.12 = (f32[3,6,16,128]{3,2,1,0:T(8,128)S(1)}, f32[3,6,16,128]{3,2,1,0:T(8,128)S(1)}, u32[]{:S(2)}, u32[]{:S(2)}) collective-permute-start(f32[3,6,16,128]{3,2,1,0:T(8,128)S(1)} %fusion.114), channel_id=1, source_target_pairs={{32,0},{64,32},{96,64},{128,96},{160,128},{192,160},{224,192},{256... | collective-permute-start | bytes 442376 | tf_op jit(solution)/shard_map/ppermute | solution.py:33
  108.3 7.0 %collective-permute-start.13 = (f32[3,6,16,128]{3,2,1,0:T(8,128)S(1)}, f32[3,6,16,128]{3,2,1,0:T(8,128)S(1)}, u32[]{:S(2)}, u32[]{:S(2)}) collective-permute-start(f32[3,6,16,128]{3,2,1,0:T(8,128)S(1)} %fusion.114), channel_id=1, source_target_pairs={{0,32},{32,64},{64,96},{96,128},{128,160},{160,192},{192,224},{224... | collective-permute-start | bytes 442376 | tf_op jit(solution)/shard_map/ppermute | solution.py:31
  115.9 8.2 %collective-permute-start.14 = (f32[3,6,16,128]{3,2,1,0:T(8,128)S(1)}, f32[3,6,16,128]{3,2,1,0:T(8,128)S(1)}, u32[]{:S(2)}, u32[]{:S(2)}) collective-permute-start(f32[3,6,16,128]{3,2,1,0:T(8,128)S(1)} %fusion.79), channel_id=1, source_target_pairs={{32,0},{64,32},{96,64},{128,96},{160,128},{192,160},{224,192},{256... | collective-permute-start | bytes 442376 | tf_op jit(solution)/shard_map/ppermute | solution.py:33
  121.4 7.0 %collective-permute-start.15 = (f32[3,6,16,128]{3,2,1,0:T(8,128)S(1)}, f32[3,6,16,128]{3,2,1,0:T(8,128)S(1)}, u32[]{:S(2)}, u32[]{:S(2)}) collective-permute-start(f32[3,6,16,128]{3,2,1,0:T(8,128)S(1)} %fusion.79), channel_id=1, source_target_pairs={{0,32},{32,64},{64,96},{96,128},{128,160},{160,192},{192,224},{224... | collective-permute-start | bytes 442376 | tf_op jit(solution)/shard_map/ppermute | solution.py:31
  129.0 12.6 %copy-start.2 = (f32[3,6,16,128]{3,2,1,0:T(8,128)}, f32[3,6,16,128]{3,2,1,0:T(8,128)S(1)}, u32[]{:S(2)}) copy-start(f32[3,6,16,128]{3,2,1,0:T(8,128)S(1)} %fusion.44) | copy-start | bytes 442372
  129.0 8.2 %collective-permute-start.16 = (f32[3,6,16,128]{3,2,1,0:T(8,128)S(1)}, f32[3,6,16,128]{3,2,1,0:T(8,128)S(1)}, u32[]{:S(2)}, u32[]{:S(2)}) collective-permute-start(f32[3,6,16,128]{3,2,1,0:T(8,128)S(1)} %fusion.44), channel_id=1, source_target_pairs={{32,0},{64,32},{96,64},{128,96},{160,128},{192,160},{224,192},{256... | collective-permute-start | bytes 442376 | tf_op jit(solution)/shard_map/ppermute | solution.py:33
  134.5 7.0 %collective-permute-start.17 = (f32[3,6,16,128]{3,2,1,0:T(8,128)S(1)}, f32[3,6,16,128]{3,2,1,0:T(8,128)S(1)}, u32[]{:S(2)}, u32[]{:S(2)}) collective-permute-start(f32[3,6,16,128]{3,2,1,0:T(8,128)S(1)} %fusion.44), channel_id=1, source_target_pairs={{0,32},{32,64},{64,96},{96,128},{128,160},{160,192},{192,224},{224... | collective-permute-start | bytes 442376 | tf_op jit(solution)/shard_map/ppermute | solution.py:31

commit v2 on v1

--- a/solution.py
+++ b/solution.py
@@ -125,25 +125,138 @@
     return jnp.sum(got, axis=0)
 
 
+def halo_of(fields, depths, planes):
+    count = lax.axis_size("domain")
+    reach = max(depths)
+    blocks = -(-reach // planes)
+    lefts = [[] for _ in fields]
+    rights = [[] for _ in fields]
+    for shift in range(1, blocks + 1):
+        wanted = [i for i, depth in enumerate(depths) if depth > (shift - 1) * planes]
+        packed = jnp.concatenate([fields[i] for i in wanted], axis=0)
+        from_left = lax.ppermute(packed, "domain", [(i, (i + shift) % count) for i in range(count)])
+        from_right = lax.ppermute(packed, "domain", [(i, (i - shift) % count) for i in range(count)])
+        row = 0
+        for i in wanted:
+            rows = fields[i].shape[0]
+            lefts[i].insert(0, from_left[row : row + rows])
+            rights[i].append(from_right[row : row + rows])
+            row += rows
+    out = []
+    for i, depth in enumerate(depths):
+        wide = jnp.concatenate(lefts[i] + [fields[i]] + rights[i], axis=1)
+        cut = len(lefts[i]) * planes - depth
+        out.append(lax.slice_in_dim(wide, cut, wide.shape[1] - cut, axis=1))
+    return out
+
+
+def crop(field, depth):
+    return lax.slice_in_dim(field, depth, field.shape[1] - depth, axis=1)
+
+
+def laplace_inner(grid_field):
+    planes = grid_field.shape[1] - 2 * stencil_reach
+    size_y = grid_field.shape[2]
+    size_z = grid_field.shape[3]
+    inner = crop(grid_field, stencil_reach)
+    padded_yz = jnp.pad(
+        inner, ((0, 0), (0, 0), (stencil_reach, stencil_reach), (stencil_reach, stencil_reach))
+    )
+    summed = 3.0 * stencil_coeffs[0] * inner
+    for offset in range(1, stencil_reach + 1):
+        along_x = (
+            grid_field[:, stencil_reach + offset : stencil_reach + offset + planes]
+            + grid_field[:, stencil_reach - offset : stencil_reach - offset + planes]
+        )
+        along_y = (
+            padded_yz[
+                :,
+                :,
+                stencil_reach + offset : stencil_reach + offset + size_y,
+                stencil_reach : stencil_reach + size_z,
+            ]
+            + padded_yz[
+                :,
+                :,
+                stencil_reach - offset : stencil_reach - offset + size_y,
+                stencil_reach : stencil_reach + size_z,
+            ]
+        )
+        along_z = (
+            padded_yz[
+                :,
+                :,
+                stencil_reach : stencil_reach + size_y,
+                stencil_reach + offset : stencil_reach + offset + size_z,
+            ]
+            + padded_yz[
+                :,
+                :,
+                stencil_reach : stencil_reach + size_y,
+                stencil_reach - offset : stencil_reach - offset + size_z,
+            ]
+        )
+        summed = summed + stencil_coeffs[offset] * (along_x + along_y + along_z)
+    return summed
+
+
+def hamiltonian_inner(grid_field, wide_pot):
+    inner = crop(grid_field, stencil_reach)
+    cut = (wide_pot.shape[0] - inner.shape[1]) // 2
+    pot = lax.slice_in_dim(wide_pot, cut, wide_pot.shape[0] - cut, axis=0)
+    return -0.5 * laplace_inner(grid_field) + pot[None] * inner
+
+
 def body(orbitals, potential):
     local_pot = gather_potential(potential)
+    planes = orbitals.shape[1]
     half_width = (upper_bound - lower_bound) / 2.0
     centre = (upper_bound + lower_bound) / 2.0
     sigma_first = half_width / (lowest_bound - centre)
-    previous = orbitals
-    current = (apply_hamiltonian(previous, local_pot) - centre * previous) * (
-        sigma_first / half_width
-    )
+    per_phase = 3
+    applications = DEGREE + 1
+    pot_depth = stencil_reach * (per_phase - 1)
+    current, wide_pot = halo_of([orbitals, local_pot[None]], [stencil_reach * per_phase, pot_depth], planes)
+    wide_pot = wide_pot[0]
+    previous = None
     sigma_now = sigma_first
-    for degree_step in range(2, DEGREE + 1):
-        sigma_next = 1.0 / (2.0 / sigma_first - sigma_now)
-        update = (apply_hamiltonian(current, local_pot) - centre * current) * (
-            2.0 * sigma_next / half_width
-        ) - sigma_now * sigma_next * previous
-        previous = current
-        current = update
-        sigma_now = sigma_next
-    h_image = apply_hamiltonian(current, local_pot)
+    step = 0
+    h_image = None
+    while step < applications:
+        if step > 0:
+            todo = min(per_phase, applications - step)
+            if previous is not None and step < DEGREE:
+                current, previous = halo_of(
+                    [current, previous], [stencil_reach * todo, stencil_reach * (todo - 1)], planes
+                )
+            else:
+                (current,) = halo_of([current], [stencil_reach * todo], planes)
+        else:
+            todo = per_phase
+        for _ in range(todo):
+            if step == 0:
+                previous = current
+                current = (hamiltonian_inner(current, wide_pot) - centre * crop(current, stencil_reach)) * (
+                    sigma_first / half_width
+                )
+            elif step < DEGREE:
+                sigma_next = 1.0 / (2.0 / sigma_first - sigma_now)
+                inner = crop(current, stencil_reach)
+                lag = (previous.shape[1] - inner.shape[1]) // 2
+                update = (hamiltonian_inner(current, wide_pot) - centre * inner) * (
+                    2.0 * sigma_next / half_width
+                ) - sigma_now * sigma_next * crop(previous, lag)
+                previous = current
+                current = update
+                sigma_now = sigma_next
+            else:
+                h_image = hamiltonian_inner(current, wide_pot)
+            step += 1
+        if step < applications:
+            lag = (previous.shape[1] - planes) // 2
+            previous = crop(previous, lag)
+    depth = (current.shape[1] - planes) // 2
+    current = crop(current, depth)
     orb_dev = current.shape[0]
     cell_count = current.shape[1] * current.shape[2] * current.shape[3] * lax.axis_size("domain")
     totals = gram_rows(current.reshape(orb_dev, -1), h_image.reshape(orb_dev, -1))

time: 208 us -> 202 us (0.971)
  waiting for transfers between devices: 47.6 us -> 20.8 us
  other arithmetic: 5.79 us -> 15.5 us
  starting transfers between devices: 85 us -> 93.3 us
  local copies, waits for them, and re-layouts: 4.03 us -> 6.11 us
    ppermute x18, waiting for transfers between devices: 47.5 us -> 18 us  [the longest x9 12.7 us: halo_of(): lax.ppermute(packed, 'domain', [(i, (i - shift) % count) for i in range(c...]
    ppermute x18, starting transfers between devices: 76 us -> 84.2 us  [the longest x9 50.4 us: halo_of(): lax.ppermute(packed, 'domain', [(i, (i - shift) % count) for i in range(c...]
    sub x7, other arithmetic: 3.73 us -> 11.4 us  [body(): (hamiltonian_inner(current, wide_pot) - centre * inner) * (2.0 * sigma_ne...]
    all_to_all x1, blocking collectives: 24 us -> 28.8 us  [gram_rows(): got = lax.all_to_all(sent, 'domain', 0, 0, tiled=True)]
    all_to_all x1, blocking collectives: 24.1 us -> 20.2 us  [gram_rows(): got = lax.all_to_all(both, 'band', 0, 0, tiled=True)]
    all_to_all x1, waiting for transfers between devices: 0.01 us -> 2.84 us  [gather_potential(): got = lax.all_to_all(sent, 'band', 0, 0, tiled=True)]
    unnamed x12 -> x32, local copies, waits for them, and re-layouts: 2.64 us -> 4.5 us
  transfers between devices with their start and end apart: 19 -> 19, of which waited for: 17 -> 10; matrix products, arithmetic and copies ran while one was open for 1% -> 2% of each run, Pallas kernels for 0% -> 0%
where the time goes in v2:
time: 202 us; the launch traced here: 201 us
  starting transfers between devices  93.3 us (46%)
  blocking collectives  63.6 us (31%)
  waiting for transfers between devices  20.8 us (10%)
  other arithmetic  15.5 us (8%)
  local copies, waits for them, and re-layouts  6.11 us (3%)
    ppermute x9, starting transfers between devices, halo_of(): lax.ppermute(packed, 'domain', [(i, (i - shift) % count) for i in range(c...  50.4 us
    ppermute x9, starting transfers between devices, halo_of(): lax.ppermute(packed, 'domain', [(i, (i + shift) % count) for i in range(c...  33.8 us
    all_to_all x1, blocking collectives, gram_rows(): got = lax.all_to_all(sent, 'domain', 0, 0, tiled=True)  28.8 us
    all_to_all x1, blocking collectives, gram_rows(): got = lax.all_to_all(both, 'band', 0, 0, tiled=True)  20.2 us
    all_to_all x1, blocking collectives, gram_rows(): got = lax.all_to_all(tiles.transpose(1, 0, 2, 3), 'band', 0, 0, tiled=True)  14.6 us
    ppermute x9, waiting for transfers between devices, halo_of(): lax.ppermute(packed, 'domain', [(i, (i - shift) % count) for i in range(c...  12.7 us
    sub x7, other arithmetic, body(): (hamiltonian_inner(current, wide_pot) - centre * inner) * (2.0 * sigma_ne...  11.4 us
    all_to_all x1, starting transfers between devices, gather_potential(): got = lax.all_to_all(sent, 'band', 0, 0, tiled=True)  9.05 us
  transfers between devices with their start and end apart: 19, of which 10 were waited for; matrix products, arithmetic and copies ran while one was open for 2% of the time, Pallas kernels for 0%

profile of v2, /device:TPU:2, one launch (start us, length us, event | category | flops | bytes accessed | tf_op | source)
XLA Modules:
  0.0 201.2 jit_solution(5820093170087330738)
XLA Ops:
  2.3 9.1 %all-to-all-start = ((f32[32,1,384]{2,1,0:T(1,128)}), f32[32,1,384]{2,1,0:T(1,128)S(1)}, u32[]{:S(2)}, u32[]{:S(2)}) async-start(f32[32,1,384]{2,1,0:T(1,128)} %reshape.46), calls=%async_computation | async-start | bytes 98304 | tf_op jit(solution)/shard_map/all_to_all | solution.py:103
  11.4 7.0 %collective-permute-start.5 = (f32[3,6,16,128]{3,2,1,0:T(8,128)S(1)}, f32[3,6,16,128]{3,2,1,0:T(8,128)S(1)}, u32[]{:S(2)}, u32[]{:S(2)}) collective-permute-start(f32[3,6,16,128]{3,2,1,0:T(8,128)S(1)} %copy-done.1), channel_id=1, source_target_pairs={{0,96},{32,128},{64,160},{96,192},{128,224},{160,256},{192,288},{2... | collective-permute-start | bytes 442376 | tf_op jit(solution)/shard_map/ppermute | solution.py:137
  18.4 2.8 %all-to-all-done = f32[32,1,384]{2,1,0:T(1,128)S(1)} async-done(((f32[32,1,384]{2,1,0:T(1,128)}), f32[32,1,384]{2,1,0:T(1,128)S(1)}, u32[]{:S(2)}, u32[]{:S(2)}) %all-to-all-start) | async-done | bytes 49184 | tf_op jit(solution)/shard_map/all_to_all | solution.py:103
  23.1 4.3 %collective-permute-start = (f32[4,6,16,128]{3,2,1,0:T(8,128)S(1)}, f32[4,6,16,128]{3,2,1,0:T(8,128)S(1)}, u32[]{:S(2)}, u32[]{:S(2)}) collective-permute-start(f32[4,6,16,128]{3,2,1,0:T(8,128)S(1)} %pad_maximum_fusion.2), channel_id=1, source_target_pairs={{0,64},{32,96},{64,128},{96,160},{128,192},{160,224},{192,256},{22... | collective-permute-start | bytes 589832 | tf_op jit(solution)/shard_map/ppermute | solution.py:137
  27.4 16.9 %collective-permute-start.4 = (f32[3,6,16,128]{3,2,1,0:T(8,128)S(1)}, f32[3,6,16,128]{3,2,1,0:T(8,128)S(1)}, u32[]{:S(2)}, u32[]{:S(2)}) collective-permute-start(f32[3,6,16,128]{3,2,1,0:T(8,128)S(1)} %copy-done.1), channel_id=1, source_target_pairs={{0,928},{32,960},{64,992},{96,0},{128,32},{160,64},{192,96},{224,1... | collective-permute-start | bytes 442376 | tf_op jit(solution)/shard_map/ppermute | solution.py:138
  44.2 3.3 %collective-permute-start.1 = (f32[4,6,16,128]{3,2,1,0:T(8,128)S(1)}, f32[4,6,16,128]{3,2,1,0:T(8,128)S(1)}, u32[]{:S(2)}, u32[]{:S(2)}) collective-permute-start(f32[4,6,16,128]{3,2,1,0:T(8,128)S(1)} %pad_maximum_fusion.2), channel_id=1, source_target_pairs={{0,32},{32,64},{64,96},{96,128},{128,160},{160,192},{192,224},{224... | collective-permute-start | bytes 589832 | tf_op jit(solution)/shard_map/ppermute | solution.py:137
  47.5 2.6 %collective-permute-start.2 = (f32[4,6,16,128]{3,2,1,0:T(8,128)S(1)}, f32[4,6,16,128]{3,2,1,0:T(8,128)S(1)}, u32[]{:S(2)}, u32[]{:S(2)}) collective-permute-start(f32[4,6,16,128]{3,2,1,0:T(8,128)S(1)} %pad_maximum_fusion.2), channel_id=1, source_target_pairs={{0,992},{32,0},{64,32},{96,64},{128,96},{160,128},{192,160},{224,1... | collective-permute-start | bytes 589832 | tf_op jit(solution)/shard_map/ppermute | solution.py:138
  50.2 4.5 %collective-permute-start.3 = (f32[4,6,16,128]{3,2,1,0:T(8,128)S(1)}, f32[4,6,16,128]{3,2,1,0:T(8,128)S(1)}, u32[]{:S(2)}, u32[]{:S(2)}) collective-permute-start(f32[4,6,16,128]{3,2,1,0:T(8,128)S(1)} %pad_maximum_fusion.2), channel_id=1, source_target_pairs={{0,960},{32,992},{64,0},{96,32},{128,64},{160,96},{192,128},{224,1... | collective-permute-start | bytes 589832 | tf_op jit(solution)/shard_map/ppermute | solution.py:138
  65.3 3.0 %collective-permute-start.11 = (f32[3,6,16,128]{3,2,1,0:T(8,128)S(1)}, f32[3,6,16,128]{3,2,1,0:T(8,128)S(1)}, u32[]{:S(2)}, u32[]{:S(2)}) collective-permute-start(f32[3,6,16,128]{3,2,1,0:T(8,128)S(1)} %fusion.355), channel_id=1, source_target_pairs={{0,96},{32,128},{64,160},{96,192},{128,224},{160,256},{192,288},{2... | collective-permute-start | bytes 442376 | tf_op jit(solution)/shard_map/ppermute | solution.py:137
  68.3 3.4 %collective-permute-start.7 = (f32[6,6,16,128]{3,2,1,0:T(8,128)S(1)}, f32[6,6,16,128]{3,2,1,0:T(8,128)S(1)}, u32[]{:S(2)}, u32[]{:S(2)}) collective-permute-start(f32[6,6,16,128]{3,2,1,0:T(8,128)S(1)} %pad_maximum_fusion), channel_id=1, source_target_pairs={{0,32},{32,64},{64,96},{96,128},{128,160},{160,192},{192,224},{224... | collective-permute-start | bytes 884744 | tf_op jit(solution)/shard_map/ppermute | solution.py:137
  71.7 2.9 %collective-permute-start.8 = (f32[6,6,16,128]{3,2,1,0:T(8,128)S(1)}, f32[6,6,16,128]{3,2,1,0:T(8,128)S(1)}, u32[]{:S(2)}, u32[]{:S(2)}) collective-permute-start(f32[6,6,16,128]{3,2,1,0:T(8,128)S(1)} %pad_maximum_fusion), channel_id=1, source_target_pairs={{0,992},{32,0},{64,32},{96,64},{128,96},{160,128},{192,160},{224,1... | collective-permute-start | bytes 884744 | tf_op jit(solution)/shard_map/ppermute | solution.py:138
  74.7 5.6 %collective-permute-start.9 = (f32[6,6,16,128]{3,2,1,0:T(8,128)S(1)}, f32[6,6,16,128]{3,2,1,0:T(8,128)S(1)}, u32[]{:S(2)}, u32[]{:S(2)}) collective-permute-start(f32[6,6,16,128]{3,2,1,0:T(8,128)S(1)} %pad_maximum_fusion), channel_id=1, source_target_pairs={{0,960},{32,992},{64,0},{96,32},{128,64},{160,96},{192,128},{224,1... | collective-permute-start | bytes 884744 | tf_op jit(solution)/shard_map/ppermute | solution.py:138
  82.2 4.4 %collective-permute-start.10 = (f32[3,6,16,128]{3,2,1,0:T(8,128)S(1)}, f32[3,6,16,128]{3,2,1,0:T(8,128)S(1)}, u32[]{:S(2)}, u32[]{:S(2)}) collective-permute-start(f32[3,6,16,128]{3,2,1,0:T(8,128)S(1)} %fusion.355), channel_id=1, source_target_pairs={{0,928},{32,960},{64,992},{96,0},{128,32},{160,64},{192,96},{224,1... | collective-permute-start | bytes 442376 | tf_op jit(solution)/shard_map/ppermute | solution.py:138
  88.1 3.7 %collective-permute-done.8 = f32[6,6,16,128]{3,2,1,0:T(8,128)S(1)} collective-permute-done((f32[6,6,16,128]{3,2,1,0:T(8,128)S(1)}, f32[6,6,16,128]{3,2,1,0:T(8,128)S(1)}, u32[]{:S(2)}, u32[]{:S(2)}) %collective-permute-start.8) | collective-permute-done | bytes 294944 | tf_op jit(solution)/shard_map/ppermute | solution.py:138
  92.1 4.2 %collective-permute-done.10 = f32[3,6,16,128]{3,2,1,0:T(8,128)S(1)} collective-permute-done((f32[3,6,16,128]{3,2,1,0:T(8,128)S(1)}, f32[3,6,16,128]{3,2,1,0:T(8,128)S(1)}, u32[]{:S(2)}, u32[]{:S(2)}) %collective-permute-start.10) | collective-permute-done | bytes 147488 | tf_op jit(solution)/shard_map/ppermute | solution.py:138
  96.3 2.6 %multiply_subtract_fusion.1 = f32[3,30,16,128]{3,2,1,0:T(8,128)S(1)} fusion(f32[3,30,16,128]{3,2,1,0:T(8,128)S(1)} %get-tuple-element.35, f32[3,30,16,128]{3,2,1,0:T(8,128)S(1)} %get-tuple-element.36, f32[3,30,16,128]{3,2,1,0:T(8,128)S(1)} %get-tuple-element.90, f32[3,30,16,128]{3,2,1,0:T(8,128)S(1)} %get-tuple-element.41, ...), kind=kLoop, calls=%fused_computation.351 | loop fusion | flops 9400320 | bytes 11304960 | tf_op jit(solution)/shard_map/sub | solution.py:246
  101.2 2.8 %collective-permute-start.12 = (f32[6,6,16,128]{3,2,1,0:T(8,128)S(1)}, f32[6,6,16,128]{3,2,1,0:T(8,128)S(1)}, u32[]{:S(2)}, u32[]{:S(2)}) collective-permute-start(f32[6,6,16,128]{3,2,1,0:T(8,128)S(1)} %pad_maximum_fusion.1), channel_id=1, source_target_pairs={{0,64},{32,96},{64,128},{96,160},{128,192},{160,224},{192,256},{22... | collective-permute-start | bytes 884744 | tf_op jit(solution)/shard_map/ppermute | solution.py:137
  106.0 6.2 %collective-permute-start.13 = (f32[6,6,16,128]{3,2,1,0:T(8,128)S(1)}, f32[6,6,16,128]{3,2,1,0:T(8,128)S(1)}, u32[]{:S(2)}, u32[]{:S(2)}) collective-permute-start(f32[6,6,16,128]{3,2,1,0:T(8,128)S(1)} %pad_maximum_fusion.1), channel_id=1, source_target_pairs={{0,32},{32,64},{64,96},{96,128},{128,160},{160,192},{192,224},{224... | collective-permute-start | bytes 884744 | tf_op jit(solution)/shard_map/ppermute | solution.py:137
  116.4 9.4 %collective-permute-start.16 = (f32[3,6,16,128]{3,2,1,0:T(8,128)S(1)}, f32[3,6,16,128]{3,2,1,0:T(8,128)S(1)}, u32[]{:S(2)}, u32[]{:S(2)}) collective-permute-start(f32[3,6,16,128]{3,2,1,0:T(8,128)S(1)} %fusion.354), channel_id=1, source_target_pairs={{0,928},{32,960},{64,992},{96,0},{128,32},{160,64},{192,96},{224,1... | collective-permute-start | bytes 442376 | tf_op jit(solution)/shard_map/ppermute | solution.py:138
  126.6 3.3 %collective-permute-done.16 = f32[3,6,16,128]{3,2,1,0:T(8,128)S(1)} collective-permute-done((f32[3,6,16,128]{3,2,1,0:T(8,128)S(1)}, f32[3,6,16,128]{3,2,1,0:T(8,128)S(1)}, u32[]{:S(2)}, u32[]{:S(2)}) %collective-permute-start.16) | collective-permute-done | bytes 147488 | tf_op jit(solution)/shard_map/ppermute | solution.py:138
  130.0 2.6 %multiply_subtract_fusion = f32[3,30,16,128]{3,2,1,0:T(8,128)S(1)} fusion(f32[3,30,16,128]{3,2,1,0:T(8,128)S(1)} %get-tuple-element.11, f32[3,30,16,128]{3,2,1,0:T(8,128)S(1)} %get-tuple-element.12, f32[3,30,16,128]{3,2,1,0:T(8,128)S(1)} %get-tuple-element.81, f32[3,30,16,128]{3,2,1,0:T(8,128)S(1)} %get-tuple-element.17, ...), kind=kLoop, calls=%fused_computation.350 | loop fusion | flops 9400320 | bytes 11304960 | tf_op jit(solution)/shard_map/sub | solution.py:246
  135.4 20.2 %all_to_all.20 = f32[32,6,384]{2,1,0:T(8,128)S(1)} all-to-all(f32[32,6,384]{2,1,0:T(8,128)S(1)} %maximum_bitcast_fusion), channel_id=1, replica_groups=mesh['domain'=32,'band'=32] {'band'}, dimensions={0} | all-to-all | bytes 589824 | tf_op jit(solution)/shard_map/all_to_all | solution.py:114
  156.5 14.6 %all_to_all.21 = f32[32,2,3,96]{3,1,2,0:T(2,128)S(1)} all-to-all(f32[32,2,3,96]{3,1,2,0:T(2,128)S(1)} %copy.43), channel_id=1, replica_groups=mesh['domain'=32,'band'=32] {'band'}, dimensions={0} | all-to-all | bytes 147456 | tf_op jit(solution)/shard_map/all_to_all | solution.py:120
  171.2 28.8 %all_to_all.22 = f32[32,2,3,96]{3,1,2,0:T(2,128)S(1)} all-to-all(f32[32,2,3,96]{3,1,2,0:T(2,128)S(1)} %broadcast_in_dim.5), channel_id=1, replica_groups=mesh['domain'=32,'band'=32] {'domain'}, dimensions={0} | all-to-all | bytes 147456 | tf_op jit(solution)/shard_map/all_to_all | solution.py:124
  (95 shorter events, 32.0 us)
Async XLA Ops:
  0.6 0.7 copy-start
  1.3 10.1 %copy-start.1 = (f32[3,6,16,128]{3,2,1,0:T(8,128)S(1)}, f32[3,6,16,128]{3,2,1,0:T(8,128)}, u32[]{:S(2)}) copy-start(f32[3,6,16,128]{3,2,1,0:T(8,128)} %param.2) | copy-start | bytes 442372
  2.3 18.9 %all-to-all-start = ((f32[32,1,384]{2,1,0:T(1,128)}), f32[32,1,384]{2,1,0:T(1,128)S(1)}, u32[]{:S(2)}, u32[]{:S(2)}) async-start(f32[32,1,384]{2,1,0:T(1,128)} %reshape.46), calls=%async_computation | async-start | bytes 98304 | tf_op jit(solution)/shard_map/all_to_all | solution.py:103
  11.4 38.8 %collective-permute-start.5 = (f32[3,6,16,128]{3,2,1,0:T(8,128)S(1)}, f32[3,6,16,128]{3,2,1,0:T(8,128)S(1)}, u32[]{:S(2)}, u32[]{:S(2)}) collective-permute-start(f32[3,6,16,128]{3,2,1,0:T(8,128)S(1)} %copy-done.1), channel_id=1, source_target_pairs={{0,96},{32,128},{64,160},{96,192},{128,224},{160,256},{192,288},{2... | collective-permute-start | bytes 442376 | tf_op jit(solution)/shard_map/ppermute | solution.py:137
  23.1 31.7 %collective-permute-start = (f32[4,6,16,128]{3,2,1,0:T(8,128)S(1)}, f32[4,6,16,128]{3,2,1,0:T(8,128)S(1)}, u32[]{:S(2)}, u32[]{:S(2)}) collective-permute-start(f32[4,6,16,128]{3,2,1,0:T(8,128)S(1)} %pad_maximum_fusion.2), channel_id=1, source_target_pairs={{0,64},{32,96},{64,128},{96,160},{128,192},{160,224},{192,256},{22... | collective-permute-start | bytes 589832 | tf_op jit(solution)/shard_map/ppermute | solution.py:137
  27.4 31.0 %collective-permute-start.4 = (f32[3,6,16,128]{3,2,1,0:T(8,128)S(1)}, f32[3,6,16,128]{3,2,1,0:T(8,128)S(1)}, u32[]{:S(2)}, u32[]{:S(2)}) collective-permute-start(f32[3,6,16,128]{3,2,1,0:T(8,128)S(1)} %copy-done.1), channel_id=1, source_target_pairs={{0,928},{32,960},{64,992},{96,0},{128,32},{160,64},{192,96},{224,1... | collective-permute-start | bytes 442376 | tf_op jit(solution)/shard_map/ppermute | solution.py:138
  44.2 12.6 %collective-permute-start.1 = (f32[4,6,16,128]{3,2,1,0:T(8,128)S(1)}, f32[4,6,16,128]{3,2,1,0:T(8,128)S(1)}, u32[]{:S(2)}, u32[]{:S(2)}) collective-permute-start(f32[4,6,16,128]{3,2,1,0:T(8,128)S(1)} %pad_maximum_fusion.2), channel_id=1, source_target_pairs={{0,32},{32,64},{64,96},{96,128},{128,160},{160,192},{192,224},{224... | collective-permute-start | bytes 589832 | tf_op jit(solution)/shard_map/ppermute | solution.py:137
  47.5 10.6 %collective-permute-start.2 = (f32[4,6,16,128]{3,2,1,0:T(8,128)S(1)}, f32[4,6,16,128]{3,2,1,0:T(8,128)S(1)}, u32[]{:S(2)}, u32[]{:S(2)}) collective-permute-start(f32[4,6,16,128]{3,2,1,0:T(8,128)S(1)} %pad_maximum_fusion.2), channel_id=1, source_target_pairs={{0,992},{32,0},{64,32},{96,64},{128,96},{160,128},{192,160},{224,1... | collective-permute-start | bytes 589832 | tf_op jit(solution)/shard_map/ppermute | solution.py:138
  50.2 8.1 %collective-permute-start.3 = (f32[4,6,16,128]{3,2,1,0:T(8,128)S(1)}, f32[4,6,16,128]{3,2,1,0:T(8,128)S(1)}, u32[]{:S(2)}, u32[]{:S(2)}) collective-permute-start(f32[4,6,16,128]{3,2,1,0:T(8,128)S(1)} %pad_maximum_fusion.2), channel_id=1, source_target_pairs={{0,960},{32,992},{64,0},{96,32},{128,64},{160,96},{192,128},{224,1... | collective-permute-start | bytes 589832 | tf_op jit(solution)/shard_map/ppermute | solution.py:138
  63.3 23.2 %collective-permute-start.6 = (f32[6,6,16,128]{3,2,1,0:T(8,128)S(1)}, f32[6,6,16,128]{3,2,1,0:T(8,128)S(1)}, u32[]{:S(2)}, u32[]{:S(2)}) collective-permute-start(f32[6,6,16,128]{3,2,1,0:T(8,128)S(1)} %pad_maximum_fusion), channel_id=1, source_target_pairs={{0,64},{32,96},{64,128},{96,160},{128,192},{160,224},{192,256},{22... | collective-permute-start | bytes 884744 | tf_op jit(solution)/shard_map/ppermute | solution.py:137
  65.3 16.8 %collective-permute-start.11 = (f32[3,6,16,128]{3,2,1,0:T(8,128)S(1)}, f32[3,6,16,128]{3,2,1,0:T(8,128)S(1)}, u32[]{:S(2)}, u32[]{:S(2)}) collective-permute-start(f32[3,6,16,128]{3,2,1,0:T(8,128)S(1)} %fusion.355), channel_id=1, source_target_pairs={{0,96},{32,128},{64,160},{96,192},{128,224},{160,256},{192,288},{2... | collective-permute-start | bytes 442376 | tf_op jit(solution)/shard_map/ppermute | solution.py:137
  68.3 19.6 %collective-permute-start.7 = (f32[6,6,16,128]{3,2,1,0:T(8,128)S(1)}, f32[6,6,16,128]{3,2,1,0:T(8,128)S(1)}, u32[]{:S(2)}, u32[]{:S(2)}) collective-permute-start(f32[6,6,16,128]{3,2,1,0:T(8,128)S(1)} %pad_maximum_fusion), channel_id=1, source_target_pairs={{0,32},{32,64},{64,96},{96,128},{128,160},{160,192},{192,224},{224... | collective-permute-start | bytes 884744 | tf_op jit(solution)/shard_map/ppermute | solution.py:137
  71.7 20.1 %collective-permute-start.8 = (f32[6,6,16,128]{3,2,1,0:T(8,128)S(1)}, f32[6,6,16,128]{3,2,1,0:T(8,128)S(1)}, u32[]{:S(2)}, u32[]{:S(2)}) collective-permute-start(f32[6,6,16,128]{3,2,1,0:T(8,128)S(1)} %pad_maximum_fusion), channel_id=1, source_target_pairs={{0,992},{32,0},{64,32},{96,64},{128,96},{160,128},{192,160},{224,1... | collective-permute-start | bytes 884744 | tf_op jit(solution)/shard_map/ppermute | solution.py:138
  74.7 17.3 %collective-permute-start.9 = (f32[6,6,16,128]{3,2,1,0:T(8,128)S(1)}, f32[6,6,16,128]{3,2,1,0:T(8,128)S(1)}, u32[]{:S(2)}, u32[]{:S(2)}) collective-permute-start(f32[6,6,16,128]{3,2,1,0:T(8,128)S(1)} %pad_maximum_fusion), channel_id=1, source_target_pairs={{0,960},{32,992},{64,0},{96,32},{128,64},{160,96},{192,128},{224,1... | collective-permute-start | bytes 884744 | tf_op jit(solution)/shard_map/ppermute | solution.py:138
  82.2 14.1 %collective-permute-start.10 = (f32[3,6,16,128]{3,2,1,0:T(8,128)S(1)}, f32[3,6,16,128]{3,2,1,0:T(8,128)S(1)}, u32[]{:S(2)}, u32[]{:S(2)}) collective-permute-start(f32[3,6,16,128]{3,2,1,0:T(8,128)S(1)} %fusion.355), channel_id=1, source_target_pairs={{0,928},{32,960},{64,992},{96,0},{128,32},{160,64},{192,96},{224,1... | collective-permute-start | bytes 442376 | tf_op jit(solution)/shard_map/ppermute | solution.py:138
  101.2 24.6 %collective-permute-start.12 = (f32[6,6,16,128]{3,2,1,0:T(8,128)S(1)}, f32[6,6,16,128]{3,2,1,0:T(8,128)S(1)}, u32[]{:S(2)}, u32[]{:S(2)}) collective-permute-start(f32[6,6,16,128]{3,2,1,0:T(8,128)S(1)} %pad_maximum_fusion.1), channel_id=1, source_target_pairs={{0,64},{32,96},{64,128},{96,160},{128,192},{160,224},{192,256},{22... | collective-permute-start | bytes 884744 | tf_op jit(solution)/shard_map/ppermute | solution.py:137
  104.0 12.4 %collective-permute-start.17 = (f32[3,6,16,128]{3,2,1,0:T(8,128)S(1)}, f32[3,6,16,128]{3,2,1,0:T(8,128)S(1)}, u32[]{:S(2)}, u32[]{:S(2)}) collective-permute-start(f32[3,6,16,128]{3,2,1,0:T(8,128)S(1)} %fusion.354), channel_id=1, source_target_pairs={{0,96},{32,128},{64,160},{96,192},{128,224},{160,256},{192,288},{2... | collective-permute-start | bytes 442376 | tf_op jit(solution)/shard_map/ppermute | solution.py:137
  106.0 20.0 %collective-permute-start.13 = (f32[6,6,16,128]{3,2,1,0:T(8,128)S(1)}, f32[6,6,16,128]{3,2,1,0:T(8,128)S(1)}, u32[]{:S(2)}, u32[]{:S(2)}) collective-permute-start(f32[6,6,16,128]{3,2,1,0:T(8,128)S(1)} %pad_maximum_fusion.1), channel_id=1, source_target_pairs={{0,32},{32,64},{64,96},{96,128},{128,160},{160,192},{192,224},{224... | collective-permute-start | bytes 884744 | tf_op jit(solution)/shard_map/ppermute | solution.py:137
  112.1 14.3 %collective-permute-start.14 = (f32[6,6,16,128]{3,2,1,0:T(8,128)S(1)}, f32[6,6,16,128]{3,2,1,0:T(8,128)S(1)}, u32[]{:S(2)}, u32[]{:S(2)}) collective-permute-start(f32[6,6,16,128]{3,2,1,0:T(8,128)S(1)} %pad_maximum_fusion.1), channel_id=1, source_target_pairs={{0,992},{32,0},{64,32},{96,64},{128,96},{160,128},{192,160},{224,1... | collective-permute-start | bytes 884744 | tf_op jit(solution)/shard_map/ppermute | solution.py:138
  114.1 12.5 %collective-permute-start.15 = (f32[6,6,16,128]{3,2,1,0:T(8,128)S(1)}, f32[6,6,16,128]{3,2,1,0:T(8,128)S(1)}, u32[]{:S(2)}, u32[]{:S(2)}) collective-permute-start(f32[6,6,16,128]{3,2,1,0:T(8,128)S(1)} %pad_maximum_fusion.1), channel_id=1, source_target_pairs={{0,960},{32,992},{64,0},{96,32},{128,64},{160,96},{192,128},{224,1... | collective-permute-start | bytes 884744 | tf_op jit(solution)/shard_map/ppermute | solution.py:138
  116.4 13.5 %collective-permute-start.16 = (f32[3,6,16,128]{3,2,1,0:T(8,128)S(1)}, f32[3,6,16,128]{3,2,1,0:T(8,128)S(1)}, u32[]{:S(2)}, u32[]{:S(2)}) collective-permute-start(f32[3,6,16,128]{3,2,1,0:T(8,128)S(1)} %fusion.354), channel_id=1, source_target_pairs={{0,928},{32,960},{64,992},{96,0},{128,32},{160,64},{192,96},{224,1... | collective-permute-start | bytes 442376 | tf_op jit(solution)/shard_map/ppermute | solution.py:138
  134.3 0.7 copy-start.2

commit v3 on v2

--- a/solution.py
+++ b/solution.py
@@ -127,26 +127,23 @@
 
 def halo_of(fields, depths, planes):
     count = lax.axis_size("domain")
-    reach = max(depths)
-    blocks = -(-reach // planes)
-    lefts = [[] for _ in fields]
-    rights = [[] for _ in fields]
-    for shift in range(1, blocks + 1):
-        wanted = [i for i, depth in enumerate(depths) if depth > (shift - 1) * planes]
-        packed = jnp.concatenate([fields[i] for i in wanted], axis=0)
-        from_left = lax.ppermute(packed, "domain", [(i, (i + shift) % count) for i in range(count)])
-        from_right = lax.ppermute(packed, "domain", [(i, (i - shift) % count) for i in range(count)])
-        row = 0
-        for i in wanted:
-            rows = fields[i].shape[0]
-            lefts[i].insert(0, from_left[row : row + rows])
-            rights[i].append(from_right[row : row + rows])
-            row += rows
+    blocks = -(-max(depths) // planes)
+    rows = [field.shape[0] for field in fields]
+    stack = jnp.concatenate(fields, axis=0)
+    have = 0
+    while have < blocks:
+        shift = 2 * have + 1
+        from_left = lax.ppermute(stack, "domain", [(i, (i + shift) % count) for i in range(count)])
+        from_right = lax.ppermute(stack, "domain", [(i, (i - shift) % count) for i in range(count)])
+        stack = jnp.concatenate([from_left, stack, from_right], axis=1)
+        have = 3 * have + 1
     out = []
-    for i, depth in enumerate(depths):
-        wide = jnp.concatenate(lefts[i] + [fields[i]] + rights[i], axis=1)
-        cut = len(lefts[i]) * planes - depth
-        out.append(lax.slice_in_dim(wide, cut, wide.shape[1] - cut, axis=1))
+    row = 0
+    for count_rows, depth in zip(rows, depths):
+        cut = have * planes - depth
+        part = stack[row : row + count_rows]
+        out.append(lax.slice_in_dim(part, cut, part.shape[1] - cut, axis=1))
+        row += count_rows
     return out
 
 
@@ -213,7 +210,7 @@
     half_width = (upper_bound - lower_bound) / 2.0
     centre = (upper_bound + lower_bound) / 2.0
     sigma_first = half_width / (lowest_bound - centre)
-    per_phase = 3
+    per_phase = 4
     applications = DEGREE + 1
     pot_depth = stencil_reach * (per_phase - 1)
     current, wide_pot = halo_of([orbitals, local_pot[None]], [stencil_reach * per_phase, pot_depth], planes)

time: 202 us -> 236 us (1.17)
  waiting for transfers between devices: 20.8 us -> 89.1 us
  starting transfers between devices: 93.3 us -> 47.9 us
  blocking collectives: 63.6 us -> 74.8 us
  other arithmetic: 15.5 us -> 17.9 us
    ppermute x18 -> x10, waiting for transfers between devices: 18 us -> 89.1 us  [the longest x5 71.9 us: halo_of(): lax.ppermute(stack, 'domain', [(i, (i + shift) % count) for i in range(co...]
    ppermute x18 -> x10, starting transfers between devices: 84.2 us -> 47.9 us  [the longest x5 33 us: halo_of(): lax.ppermute(stack, 'domain', [(i, (i - shift) % count) for i in range(co...]
    all_to_all x0 -> x1, blocking collectives: none -> 18.7 us  [gather_potential(): got = lax.all_to_all(sent, 'band', 0, 0, tiled=True)]
    all_to_all x1 -> x0, starting transfers between devices: 9.05 us -> none  [gather_potential(): got = lax.all_to_all(sent, 'band', 0, 0, tiled=True)]
    all_to_all x1, blocking collectives: 28.8 us -> 23.2 us  [gram_rows(): got = lax.all_to_all(sent, 'domain', 0, 0, tiled=True)]
    all_to_all x1 -> x0, waiting for transfers between devices: 2.84 us -> none  [gather_potential(): got = lax.all_to_all(sent, 'band', 0, 0, tiled=True)]
  transfers between devices with their start and end apart: 19 -> 10, of which waited for: 10 -> 10; matrix products, arithmetic and copies ran while one was open for 2% -> 0% of each run, Pallas kernels for 0% -> 0%
where the time goes in v3:
time: 236 us; the launch traced here: 235 us
  waiting for transfers between devices  89.1 us (38%)
  blocking collectives  74.8 us (32%)
  starting transfers between devices  47.9 us (20%)
  other arithmetic  17.9 us (8%)
  local copies, waits for them, and re-layouts  4 us (2%)
    ppermute x5, waiting for transfers between devices, halo_of(): lax.ppermute(stack, 'domain', [(i, (i + shift) % count) for i in range(co...  71.9 us
    ppermute x5, starting transfers between devices, halo_of(): lax.ppermute(stack, 'domain', [(i, (i - shift) % count) for i in range(co...  33 us
    all_to_all x1, blocking collectives, gram_rows(): got = lax.all_to_all(sent, 'domain', 0, 0, tiled=True)  23.2 us
    all_to_all x1, blocking collectives, gather_potential(): got = lax.all_to_all(sent, 'band', 0, 0, tiled=True)  18.7 us
    all_to_all x1, blocking collectives, gram_rows(): got = lax.all_to_all(both, 'band', 0, 0, tiled=True)  18.4 us
    ppermute x5, waiting for transfers between devices, halo_of(): lax.ppermute(stack, 'domain', [(i, (i - shift) % count) for i in range(co...  17.1 us
    ppermute x5, starting transfers between devices, halo_of(): lax.ppermute(stack, 'domain', [(i, (i + shift) % count) for i in range(co...  15 us
    all_to_all x1, blocking collectives, gram_rows(): got = lax.all_to_all(tiles.transpose(1, 0, 2, 3), 'band', 0, 0, tiled=True)  14.5 us
  transfers between devices with their start and end apart: 10, of which 10 were waited for; matrix products, arithmetic and copies ran while one was open for 0% of the time, Pallas kernels for 0%

profile of v3, /device:TPU:2, one launch (start us, length us, event | category | flops | bytes accessed | tf_op | source)
XLA Modules:
  0.0 235.4 jit_solution(4636663527566494926)
XLA Ops:
  1.7 18.7 %all_to_all.20 = f32[32,1,384]{2,1,0:T(1,128)S(1)} all-to-all(f32[32,1,384]{2,1,0:T(1,128)S(1)} %reshape.48), channel_id=1, replica_groups=mesh['domain'=32,'band'=32] {'band'}, dimensions={0} | all-to-all | bytes 98304 | tf_op jit(solution)/shard_map/all_to_all | solution.py:103
  22.3 9.2 %collective-permute-start.1 = (f32[4,6,16,128]{3,2,1,0:T(8,128)S(1)}, f32[4,6,16,128]{3,2,1,0:T(8,128)S(1)}, u32[]{:S(2)}, u32[]{:S(2)}) collective-permute-start(f32[4,6,16,128]{3,2,1,0:T(8,128)S(1)} %pad_maximum_fusion.3), channel_id=1, source_target_pairs={{0,992},{32,0},{64,32},{96,64},{128,96},{160,128},{192,160},{224,1... | collective-permute-start | bytes 589832 | tf_op jit(solution)/shard_map/ppermute | solution.py:137
  33.4 2.5 %collective-permute-done.1 = f32[4,6,16,128]{3,2,1,0:T(8,128)S(1)} collective-permute-done((f32[4,6,16,128]{3,2,1,0:T(8,128)S(1)}, f32[4,6,16,128]{3,2,1,0:T(8,128)S(1)}, u32[]{:S(2)}, u32[]{:S(2)}) %collective-permute-start.1) | collective-permute-done | bytes 196640 | tf_op jit(solution)/shard_map/ppermute | solution.py:137
  35.9 12.8 %collective-permute-done = f32[4,6,16,128]{3,2,1,0:T(8,128)S(1)} collective-permute-done((f32[4,6,16,128]{3,2,1,0:T(8,128)S(1)}, f32[4,6,16,128]{3,2,1,0:T(8,128)S(1)}, u32[]{:S(2)}, u32[]{:S(2)}) %collective-permute-start) | collective-permute-done | bytes 196640 | tf_op jit(solution)/shard_map/ppermute | solution.py:136
  50.9 6.0 %collective-permute-start.3 = (f32[4,18,16,128]{3,2,1,0:T(8,128)S(1)}, f32[4,18,16,128]{3,2,1,0:T(8,128)S(1)}, u32[]{:S(2)}, u32[]{:S(2)}) collective-permute-start(f32[4,18,16,128]{3,2,1,0:T(8,128)S(1)} %pad_maximum_fusion.1), channel_id=1, source_target_pairs={{0,928},{32,960},{64,992},{96,0},{128,32},{160,64},{192,96},{224,1... | collective-permute-start | bytes 1769480 | tf_op jit(solution)/shard_map/ppermute | solution.py:137
  56.9 19.0 %collective-permute-done.2 = f32[4,18,16,128]{3,2,1,0:T(8,128)S(1)} collective-permute-done((f32[4,18,16,128]{3,2,1,0:T(8,128)S(1)}, f32[4,18,16,128]{3,2,1,0:T(8,128)S(1)}, u32[]{:S(2)}, u32[]{:S(2)}) %collective-permute-start.2) | collective-permute-done | bytes 589856 | tf_op jit(solution)/shard_map/ppermute | solution.py:136
  76.1 4.7 %collective-permute-done.3 = f32[4,18,16,128]{3,2,1,0:T(8,128)S(1)} collective-permute-done((f32[4,18,16,128]{3,2,1,0:T(8,128)S(1)}, f32[4,18,16,128]{3,2,1,0:T(8,128)S(1)}, u32[]{:S(2)}, u32[]{:S(2)}) %collective-permute-start.3) | collective-permute-done | bytes 589856 | tf_op jit(solution)/shard_map/ppermute | solution.py:137
  81.0 3.4 %fusion.79 = f32[3,42,16,128]{3,2,1,0:T(8,128)S(1)} fusion(f32[3,42,16,128]{3,2,1,0:T(8,128)S(1)} %slice.1450, f32[4,54,16,128]{3,2,1,0:T(8,128)S(1)} %constant_dynamic-update-slice_fusion, f32[42,16,128]{2,1,0:T(8,128)S(1)} %slice_bitcast_fusion), kind=kLoop, calls=%fused_computation.310 | loop fusion | flops 12644352 | bytes 14794752 | tf_op jit(solution)/shard_map/mul | solution.py:236
  84.5 2.6 %fusion.159 = f32[3,30,16,128]{3,2,1,0:T(8,128)S(1)} fusion(f32[4,54,16,128]{3,2,1,0:T(8,128)S(1)} %constant_dynamic-update-slice_fusion, f32[3,30,16,128]{3,2,1,0:T(8,128)S(1)} %slice.1464, f32[3,42,16,128]{3,2,1,0:T(8,128)S(1)} %fusion.79, f32[30,16,128]{2,1,0:T(8,128)S(1)} %slice_bitcast_fusion.1), kind=kLoop, calls=%fused_computation.399 | loop fusion | flops 9400320 | bytes 11304960 | tf_op jit(solution)/shard_map/sub | solution.py:243
  89.3 6.7 %collective-permute-start.5 = (f32[6,6,16,128]{3,2,1,0:T(8,128)S(1)}, f32[6,6,16,128]{3,2,1,0:T(8,128)S(1)}, u32[]{:S(2)}, u32[]{:S(2)}) collective-permute-start(f32[6,6,16,128]{3,2,1,0:T(8,128)S(1)} %pad_maximum_fusion.2), channel_id=1, source_target_pairs={{0,992},{32,0},{64,32},{96,64},{128,96},{160,128},{192,160},{224,1... | collective-permute-start | bytes 884744 | tf_op jit(solution)/shard_map/ppermute | solution.py:137
  97.9 3.4 %collective-permute-done.5 = f32[6,6,16,128]{3,2,1,0:T(8,128)S(1)} collective-permute-done((f32[6,6,16,128]{3,2,1,0:T(8,128)S(1)}, f32[6,6,16,128]{3,2,1,0:T(8,128)S(1)}, u32[]{:S(2)}, u32[]{:S(2)}) %collective-permute-start.5) | collective-permute-done | bytes 294944 | tf_op jit(solution)/shard_map/ppermute | solution.py:137
  101.3 5.8 %collective-permute-done.4 = f32[6,6,16,128]{3,2,1,0:T(8,128)S(1)} collective-permute-done((f32[6,6,16,128]{3,2,1,0:T(8,128)S(1)}, f32[6,6,16,128]{3,2,1,0:T(8,128)S(1)}, u32[]{:S(2)}, u32[]{:S(2)}) %collective-permute-start.4) | collective-permute-done | bytes 294944 | tf_op jit(solution)/shard_map/ppermute | solution.py:136
  109.1 8.0 %collective-permute-start.7 = (f32[6,18,16,128]{3,2,1,0:T(8,128)S(1)}, f32[6,18,16,128]{3,2,1,0:T(8,128)S(1)}, u32[]{:S(2)}, u32[]{:S(2)}) collective-permute-start(f32[6,18,16,128]{3,2,1,0:T(8,128)S(1)} %pad_maximum_fusion), channel_id=1, source_target_pairs={{0,928},{32,960},{64,992},{96,0},{128,32},{160,64},{192,96},{224,1... | collective-permute-start | bytes 2654216 | tf_op jit(solution)/shard_map/ppermute | solution.py:137
  117.2 30.9 %collective-permute-done.6 = f32[6,18,16,128]{3,2,1,0:T(8,128)S(1)} collective-permute-done((f32[6,18,16,128]{3,2,1,0:T(8,128)S(1)}, f32[6,18,16,128]{3,2,1,0:T(8,128)S(1)}, u32[]{:S(2)}, u32[]{:S(2)}) %collective-permute-start.6) | collective-permute-done | bytes 884768 | tf_op jit(solution)/shard_map/ppermute | solution.py:136
  148.3 3.8 %collective-permute-done.7 = f32[6,18,16,128]{3,2,1,0:T(8,128)S(1)} collective-permute-done((f32[6,18,16,128]{3,2,1,0:T(8,128)S(1)}, f32[6,18,16,128]{3,2,1,0:T(8,128)S(1)}, u32[]{:S(2)}, u32[]{:S(2)}) %collective-permute-start.7) | collective-permute-done | bytes 884768 | tf_op jit(solution)/shard_map/ppermute | solution.py:137
  152.2 3.4 %fusion.78 = f32[3,42,16,128]{3,2,1,0:T(8,128)S(1)} fusion(f32[6,54,16,128]{3,2,1,0:T(8,128)S(1)} %constant_dynamic-update-slice_fusion.5, f32[3,42,16,128]{3,2,1,0:T(8,128)S(1)} %slice.1508, f32[42,16,128]{2,1,0:T(8,128)S(1)} %slice_bitcast_fusion), kind=kLoop, calls=%fused_computation.297 | loop fusion | flops 13160448 | bytes 15826944 | tf_op jit(solution)/shard_map/sub | solution.py:243
  155.7 2.5 %fusion.158 = f32[3,30,16,128]{3,2,1,0:T(8,128)S(1)} fusion(f32[6,54,16,128]{3,2,1,0:T(8,128)S(1)} %constant_dynamic-update-slice_fusion.5, f32[3,30,16,128]{3,2,1,0:T(8,128)S(1)} %slice.1522, f32[3,42,16,128]{3,2,1,0:T(8,128)S(1)} %fusion.78, f32[30,16,128]{2,1,0:T(8,128)S(1)} %slice_bitcast_fusion.1), kind=kLoop, calls=%fused_computation.391 | loop fusion | flops 9400320 | bytes 11304960 | tf_op jit(solution)/shard_map/sub | solution.py:243
  160.5 7.3 %collective-permute-start.9 = (f32[3,6,16,128]{3,2,1,0:T(8,128)S(1)}, f32[3,6,16,128]{3,2,1,0:T(8,128)S(1)}, u32[]{:S(2)}, u32[]{:S(2)}) collective-permute-start(f32[3,6,16,128]{3,2,1,0:T(8,128)S(1)} %fusion.369), channel_id=1, source_target_pairs={{0,32},{32,64},{64,96},{96,128},{128,160},{160,192},{192,224},{224... | collective-permute-start | bytes 442376 | tf_op jit(solution)/shard_map/ppermute | solution.py:136
  167.7 3.0 %collective-permute-start.8 = (f32[3,6,16,128]{3,2,1,0:T(8,128)S(1)}, f32[3,6,16,128]{3,2,1,0:T(8,128)S(1)}, u32[]{:S(2)}, u32[]{:S(2)}) collective-permute-start(f32[3,6,16,128]{3,2,1,0:T(8,128)S(1)} %fusion.369), channel_id=1, source_target_pairs={{0,992},{32,0},{64,32},{96,64},{128,96},{160,128},{192,160},{224,1... | collective-permute-start | bytes 442376 | tf_op jit(solution)/shard_map/ppermute | solution.py:137
  170.8 3.3 %collective-permute-done.9 = f32[3,6,16,128]{3,2,1,0:T(8,128)S(1)} collective-permute-done((f32[3,6,16,128]{3,2,1,0:T(8,128)S(1)}, f32[3,6,16,128]{3,2,1,0:T(8,128)S(1)}, u32[]{:S(2)}, u32[]{:S(2)}) %collective-permute-start.9) | collective-permute-done | bytes 147488 | tf_op jit(solution)/shard_map/ppermute | solution.py:136
  174.1 2.8 %collective-permute-done.8 = f32[3,6,16,128]{3,2,1,0:T(8,128)S(1)} collective-permute-done((f32[3,6,16,128]{3,2,1,0:T(8,128)S(1)}, f32[3,6,16,128]{3,2,1,0:T(8,128)S(1)}, u32[]{:S(2)}, u32[]{:S(2)}) %collective-permute-start.8) | collective-permute-done | bytes 147488 | tf_op jit(solution)/shard_map/ppermute | solution.py:137
  177.6 18.4 %all_to_all.21 = f32[32,6,384]{2,1,0:T(8,128)S(1)} all-to-all(f32[32,6,384]{2,1,0:T(8,128)S(1)} %copy.31), channel_id=1, replica_groups=mesh['domain'=32,'band'=32] {'band'}, dimensions={0} | all-to-all | bytes 589824 | tf_op jit(solution)/shard_map/all_to_all | solution.py:114
  196.9 14.5 %all_to_all.22 = f32[32,2,3,96]{3,1,2,0:T(2,128)S(1)} all-to-all(f32[32,2,3,96]{3,1,2,0:T(2,128)S(1)} %copy.35), channel_id=1, replica_groups=mesh['domain'=32,'band'=32] {'band'}, dimensions={0} | all-to-all | bytes 147456 | tf_op jit(solution)/shard_map/all_to_all | solution.py:120
  211.5 23.2 %all_to_all.23 = f32[32,2,3,96]{3,1,2,0:T(2,128)S(1)} all-to-all(f32[32,2,3,96]{3,1,2,0:T(2,128)S(1)} %broadcast_in_dim.5), channel_id=1, replica_groups=mesh['domain'=32,'band'=32] {'domain'}, dimensions={0} | all-to-all | bytes 147456 | tf_op jit(solution)/shard_map/all_to_all | solution.py:124
  (64 shorter events, 18.3 us)
Async XLA Ops:
  0.6 0.7 copy-start
  1.3 20.9 %copy-start.1 = (f32[3,6,16,128]{3,2,1,0:T(8,128)S(1)}, f32[3,6,16,128]{3,2,1,0:T(8,128)}, u32[]{:S(2)}) copy-start(f32[3,6,16,128]{3,2,1,0:T(8,128)} %param.2) | copy-start | bytes 442372
  22.3 13.6 %collective-permute-start.1 = (f32[4,6,16,128]{3,2,1,0:T(8,128)S(1)}, f32[4,6,16,128]{3,2,1,0:T(8,128)S(1)}, u32[]{:S(2)}, u32[]{:S(2)}) collective-permute-start(f32[4,6,16,128]{3,2,1,0:T(8,128)S(1)} %pad_maximum_fusion.3), channel_id=1, source_target_pairs={{0,992},{32,0},{64,32},{96,64},{128,96},{160,128},{192,160},{224,1... | collective-permute-start | bytes 589832 | tf_op jit(solution)/shard_map/ppermute | solution.py:137
  31.5 17.3 %collective-permute-start = (f32[4,6,16,128]{3,2,1,0:T(8,128)S(1)}, f32[4,6,16,128]{3,2,1,0:T(8,128)S(1)}, u32[]{:S(2)}, u32[]{:S(2)}) collective-permute-start(f32[4,6,16,128]{3,2,1,0:T(8,128)S(1)} %pad_maximum_fusion.3), channel_id=1, source_target_pairs={{0,32},{32,64},{64,96},{96,128},{128,160},{160,192},{192,224},{224... | collective-permute-start | bytes 589832 | tf_op jit(solution)/shard_map/ppermute | solution.py:136
  48.8 27.2 %collective-permute-start.2 = (f32[4,18,16,128]{3,2,1,0:T(8,128)S(1)}, f32[4,18,16,128]{3,2,1,0:T(8,128)S(1)}, u32[]{:S(2)}, u32[]{:S(2)}) collective-permute-start(f32[4,18,16,128]{3,2,1,0:T(8,128)S(1)} %pad_maximum_fusion.1), channel_id=1, source_target_pairs={{0,96},{32,128},{64,160},{96,192},{128,224},{160,256},{192,288},{2... | collective-permute-start | bytes 1769480 | tf_op jit(solution)/shard_map/ppermute | solution.py:136
  50.9 29.9 %collective-permute-start.3 = (f32[4,18,16,128]{3,2,1,0:T(8,128)S(1)}, f32[4,18,16,128]{3,2,1,0:T(8,128)S(1)}, u32[]{:S(2)}, u32[]{:S(2)}) collective-permute-start(f32[4,18,16,128]{3,2,1,0:T(8,128)S(1)} %pad_maximum_fusion.1), channel_id=1, source_target_pairs={{0,928},{32,960},{64,992},{96,0},{128,32},{160,64},{192,96},{224,1... | collective-permute-start | bytes 1769480 | tf_op jit(solution)/shard_map/ppermute | solution.py:137
  89.3 12.0 %collective-permute-start.5 = (f32[6,6,16,128]{3,2,1,0:T(8,128)S(1)}, f32[6,6,16,128]{3,2,1,0:T(8,128)S(1)}, u32[]{:S(2)}, u32[]{:S(2)}) collective-permute-start(f32[6,6,16,128]{3,2,1,0:T(8,128)S(1)} %pad_maximum_fusion.2), channel_id=1, source_target_pairs={{0,992},{32,0},{64,32},{96,64},{128,96},{160,128},{192,160},{224,1... | collective-permute-start | bytes 884744 | tf_op jit(solution)/shard_map/ppermute | solution.py:137
  96.0 11.2 %collective-permute-start.4 = (f32[6,6,16,128]{3,2,1,0:T(8,128)S(1)}, f32[6,6,16,128]{3,2,1,0:T(8,128)S(1)}, u32[]{:S(2)}, u32[]{:S(2)}) collective-permute-start(f32[6,6,16,128]{3,2,1,0:T(8,128)S(1)} %pad_maximum_fusion.2), channel_id=1, source_target_pairs={{0,32},{32,64},{64,96},{96,128},{128,160},{160,192},{192,224},{224... | collective-permute-start | bytes 884744 | tf_op jit(solution)/shard_map/ppermute | solution.py:136
  107.2 40.9 %collective-permute-start.6 = (f32[6,18,16,128]{3,2,1,0:T(8,128)S(1)}, f32[6,18,16,128]{3,2,1,0:T(8,128)S(1)}, u32[]{:S(2)}, u32[]{:S(2)}) collective-permute-start(f32[6,18,16,128]{3,2,1,0:T(8,128)S(1)} %pad_maximum_fusion), channel_id=1, source_target_pairs={{0,96},{32,128},{64,160},{96,192},{128,224},{160,256},{192,288},{2... | collective-permute-start | bytes 2654216 | tf_op jit(solution)/shard_map/ppermute | solution.py:136
  109.1 42.9 %collective-permute-start.7 = (f32[6,18,16,128]{3,2,1,0:T(8,128)S(1)}, f32[6,18,16,128]{3,2,1,0:T(8,128)S(1)}, u32[]{:S(2)}, u32[]{:S(2)}) collective-permute-start(f32[6,18,16,128]{3,2,1,0:T(8,128)S(1)} %pad_maximum_fusion), channel_id=1, source_target_pairs={{0,928},{32,960},{64,992},{96,0},{128,32},{160,64},{192,96},{224,1... | collective-permute-start | bytes 2654216 | tf_op jit(solution)/shard_map/ppermute | solution.py:137
  160.4 36.4 %copy-start.2 = (f32[3,6,16,128]{3,2,1,0:T(8,128)}, f32[3,6,16,128]{3,2,1,0:T(8,128)S(1)}, u32[]{:S(2)}) copy-start(f32[3,6,16,128]{3,2,1,0:T(8,128)S(1)} %fusion.369) | copy-start | bytes 442372
  160.5 13.6 %collective-permute-start.9 = (f32[3,6,16,128]{3,2,1,0:T(8,128)S(1)}, f32[3,6,16,128]{3,2,1,0:T(8,128)S(1)}, u32[]{:S(2)}, u32[]{:S(2)}) collective-permute-start(f32[3,6,16,128]{3,2,1,0:T(8,128)S(1)} %fusion.369), channel_id=1, source_target_pairs={{0,32},{32,64},{64,96},{96,128},{128,160},{160,192},{192,224},{224... | collective-permute-start | bytes 442376 | tf_op jit(solution)/shard_map/ppermute | solution.py:136
  167.7 9.1 %collective-permute-start.8 = (f32[3,6,16,128]{3,2,1,0:T(8,128)S(1)}, f32[3,6,16,128]{3,2,1,0:T(8,128)S(1)}, u32[]{:S(2)}, u32[]{:S(2)}) collective-permute-start(f32[3,6,16,128]{3,2,1,0:T(8,128)S(1)} %fusion.369), channel_id=1, source_target_pairs={{0,992},{32,0},{64,32},{96,64},{128,96},{160,128},{192,160},{224,1... | collective-permute-start | bytes 442376 | tf_op jit(solution)/shard_map/ppermute | solution.py:137

commit v4 on v2

--- a/solution.py
+++ b/solution.py
@@ -213,7 +213,7 @@
     half_width = (upper_bound - lower_bound) / 2.0
     centre = (upper_bound + lower_bound) / 2.0
     sigma_first = half_width / (lowest_bound - centre)
-    per_phase = 3
+    per_phase = 2
     applications = DEGREE + 1
     pot_depth = stencil_reach * (per_phase - 1)
     current, wide_pot = halo_of([orbitals, local_pot[None]], [stencil_reach * per_phase, pot_depth], planes)

time: 202 us -> 191 us (0.946)
  starting transfers between devices: 93.3 us -> 75.9 us
  blocking collectives: 63.6 us -> 73.5 us
  other arithmetic: 15.5 us -> 11.6 us
    all_to_all x0 -> x1, blocking collectives: none -> 18.7 us  [gather_potential(): got = lax.all_to_all(sent, 'band', 0, 0, tiled=True)]
    ppermute x9, waiting for transfers between devices: 5.26 us -> 22.7 us  [halo_of(): lax.ppermute(packed, 'domain', [(i, (i + shift) % count) for i in range(c...]
    ppermute x9, waiting for transfers between devices: 12.7 us -> 0.02 us  [halo_of(): lax.ppermute(packed, 'domain', [(i, (i - shift) % count) for i in range(c...]
    all_to_all x1 -> x0, starting transfers between devices: 9.05 us -> none  [gather_potential(): got = lax.all_to_all(sent, 'band', 0, 0, tiled=True)]
    ppermute x9, starting transfers between devices: 33.8 us -> 26 us  [halo_of(): lax.ppermute(packed, 'domain', [(i, (i + shift) % count) for i in range(c...]
    all_to_all x1, blocking collectives: 28.8 us -> 21.9 us  [gram_rows(): got = lax.all_to_all(sent, 'domain', 0, 0, tiled=True)]
    sub x7, other arithmetic: 11.4 us -> 7.71 us  [body(): (hamiltonian_inner(current, wide_pot) - centre * inner) * (2.0 * sigma_ne...]
    all_to_all x1 -> x0, waiting for transfers between devices: 2.84 us -> none  [gather_potential(): got = lax.all_to_all(sent, 'band', 0, 0, tiled=True)]
  transfers between devices with their start and end apart: 19 -> 18, of which waited for: 10 -> 8; matrix products, arithmetic and copies ran while one was open for 2% -> 0% of each run, Pallas kernels for 0% -> 0%
where the time goes in v4:
time: 191 us; the launch traced here: 190 us
  starting transfers between devices  75.9 us (40%)
  blocking collectives  73.5 us (38%)
  waiting for transfers between devices  22.7 us (12%)
  other arithmetic  11.6 us (6%)
  local copies, waits for them, and re-layouts  4.29 us (2%)
    ppermute x9, starting transfers between devices, halo_of(): lax.ppermute(packed, 'domain', [(i, (i - shift) % count) for i in range(c...  49.9 us
    ppermute x9, starting transfers between devices, halo_of(): lax.ppermute(packed, 'domain', [(i, (i + shift) % count) for i in range(c...  26 us
    ppermute x9, waiting for transfers between devices, halo_of(): lax.ppermute(packed, 'domain', [(i, (i + shift) % count) for i in range(c...  22.7 us
    all_to_all x1, blocking collectives, gram_rows(): got = lax.all_to_all(sent, 'domain', 0, 0, tiled=True)  21.9 us
    all_to_all x1, blocking collectives, gather_potential(): got = lax.all_to_all(sent, 'band', 0, 0, tiled=True)  18.7 us
    all_to_all x1, blocking collectives, gram_rows(): got = lax.all_to_all(both, 'band', 0, 0, tiled=True)  18.4 us
    all_to_all x1, blocking collectives, gram_rows(): got = lax.all_to_all(tiles.transpose(1, 0, 2, 3), 'band', 0, 0, tiled=True)  14.5 us
    sub x7, other arithmetic, body(): (hamiltonian_inner(current, wide_pot) - centre * inner) * (2.0 * sigma_ne...  7.71 us
  transfers between devices with their start and end apart: 18, of which 8 were waited for; matrix products, arithmetic and copies ran while one was open for 0% of the time, Pallas kernels for 0%

profile of v4, /device:TPU:2, one launch (start us, length us, event | category | flops | bytes accessed | tf_op | source)
XLA Modules:
  0.0 189.8 jit_solution(13768914546753726892)
XLA Ops:
  1.7 18.7 %all_to_all.20 = f32[32,1,384]{2,1,0:T(1,128)S(1)} all-to-all(f32[32,1,384]{2,1,0:T(1,128)S(1)} %reshape.44), channel_id=1, replica_groups=mesh['domain'=32,'band'=32] {'band'}, dimensions={0} | all-to-all | bytes 98304 | tf_op jit(solution)/shard_map/all_to_all | solution.py:103
  23.0 9.2 %collective-permute-start.1 = (f32[4,6,16,128]{3,2,1,0:T(8,128)S(1)}, f32[4,6,16,128]{3,2,1,0:T(8,128)S(1)}, u32[]{:S(2)}, u32[]{:S(2)}) collective-permute-start(f32[4,6,16,128]{3,2,1,0:T(8,128)S(1)} %pad_maximum_fusion.15), channel_id=1, source_target_pairs={{0,992},{32,0},{64,32},{96,64},{128,96},{160,128},{192,160},{224,1... | collective-permute-start | bytes 589832 | tf_op jit(solution)/shard_map/ppermute | solution.py:138
  32.2 1.9 %collective-permute-start = (f32[4,6,16,128]{3,2,1,0:T(8,128)S(1)}, f32[4,6,16,128]{3,2,1,0:T(8,128)S(1)}, u32[]{:S(2)}, u32[]{:S(2)}) collective-permute-start(f32[4,6,16,128]{3,2,1,0:T(8,128)S(1)} %pad_maximum_fusion.15), channel_id=1, source_target_pairs={{0,32},{32,64},{64,96},{96,128},{128,160},{160,192},{192,224},{224... | collective-permute-start | bytes 589832 | tf_op jit(solution)/shard_map/ppermute | solution.py:137
  34.1 1.9 %collective-permute-start.3 = (f32[3,6,16,128]{3,2,1,0:T(8,128)S(1)}, f32[3,6,16,128]{3,2,1,0:T(8,128)S(1)}, u32[]{:S(2)}, u32[]{:S(2)}) collective-permute-start(f32[3,6,16,128]{3,2,1,0:T(8,128)S(1)} %copy-done.1), channel_id=1, source_target_pairs={{0,64},{32,96},{64,128},{96,160},{128,192},{160,224},{192,256},{22... | collective-permute-start | bytes 442376 | tf_op jit(solution)/shard_map/ppermute | solution.py:137
  36.0 15.0 %collective-permute-start.2 = (f32[3,6,16,128]{3,2,1,0:T(8,128)S(1)}, f32[3,6,16,128]{3,2,1,0:T(8,128)S(1)}, u32[]{:S(2)}, u32[]{:S(2)}) collective-permute-start(f32[3,6,16,128]{3,2,1,0:T(8,128)S(1)} %copy-done.1), channel_id=1, source_target_pairs={{0,960},{32,992},{64,0},{96,32},{128,64},{160,96},{192,128},{224,1... | collective-permute-start | bytes 442376 | tf_op jit(solution)/shard_map/ppermute | solution.py:138
  51.4 3.6 %collective-permute-done.3 = f32[3,6,16,128]{3,2,1,0:T(8,128)S(1)} collective-permute-done((f32[3,6,16,128]{3,2,1,0:T(8,128)S(1)}, f32[3,6,16,128]{3,2,1,0:T(8,128)S(1)}, u32[]{:S(2)}, u32[]{:S(2)}) %collective-permute-start.3) | collective-permute-done | bytes 147488 | tf_op jit(solution)/shard_map/ppermute | solution.py:137
  57.5 1.9 %collective-permute-start.5 = (f32[6,6,16,128]{3,2,1,0:T(8,128)S(1)}, f32[6,6,16,128]{3,2,1,0:T(8,128)S(1)}, u32[]{:S(2)}, u32[]{:S(2)}) collective-permute-start(f32[6,6,16,128]{3,2,1,0:T(8,128)S(1)} %pad_maximum_fusion.12), channel_id=1, source_target_pairs={{0,992},{32,0},{64,32},{96,64},{128,96},{160,128},{192,160},{224,1... | collective-permute-start | bytes 884744 | tf_op jit(solution)/shard_map/ppermute | solution.py:138
  59.4 4.8 %collective-permute-start.4 = (f32[6,6,16,128]{3,2,1,0:T(8,128)S(1)}, f32[6,6,16,128]{3,2,1,0:T(8,128)S(1)}, u32[]{:S(2)}, u32[]{:S(2)}) collective-permute-start(f32[6,6,16,128]{3,2,1,0:T(8,128)S(1)} %pad_maximum_fusion.12), channel_id=1, source_target_pairs={{0,32},{32,64},{64,96},{96,128},{128,160},{160,192},{192,224},{224... | collective-permute-start | bytes 884744 | tf_op jit(solution)/shard_map/ppermute | solution.py:137
  64.2 1.9 %collective-permute-start.7 = (f32[3,6,16,128]{3,2,1,0:T(8,128)S(1)}, f32[3,6,16,128]{3,2,1,0:T(8,128)S(1)}, u32[]{:S(2)}, u32[]{:S(2)}) collective-permute-start(f32[3,6,16,128]{3,2,1,0:T(8,128)S(1)} %multiply_subtract_fusion.3), channel_id=1, source_target_pairs={{0,64},{32,96},{64,128},{96,160},{128,192},{160,224},{192,256},{22... | collective-permute-start | bytes 442376 | tf_op jit(solution)/shard_map/ppermute | solution.py:137
  66.1 5.7 %collective-permute-start.6 = (f32[3,6,16,128]{3,2,1,0:T(8,128)S(1)}, f32[3,6,16,128]{3,2,1,0:T(8,128)S(1)}, u32[]{:S(2)}, u32[]{:S(2)}) collective-permute-start(f32[3,6,16,128]{3,2,1,0:T(8,128)S(1)} %multiply_subtract_fusion.3), channel_id=1, source_target_pairs={{0,960},{32,992},{64,0},{96,32},{128,64},{160,96},{192,128},{224,1... | collective-permute-start | bytes 442376 | tf_op jit(solution)/shard_map/ppermute | solution.py:138
  71.9 2.6 %collective-permute-done.4 = f32[6,6,16,128]{3,2,1,0:T(8,128)S(1)} collective-permute-done((f32[6,6,16,128]{3,2,1,0:T(8,128)S(1)}, f32[6,6,16,128]{3,2,1,0:T(8,128)S(1)}, u32[]{:S(2)}, u32[]{:S(2)}) %collective-permute-start.4) | collective-permute-done | bytes 294944 | tf_op jit(solution)/shard_map/ppermute | solution.py:137
  80.9 4.8 %collective-permute-start.8 = (f32[6,6,16,128]{3,2,1,0:T(8,128)S(1)}, f32[6,6,16,128]{3,2,1,0:T(8,128)S(1)}, u32[]{:S(2)}, u32[]{:S(2)}) collective-permute-start(f32[6,6,16,128]{3,2,1,0:T(8,128)S(1)} %pad_maximum_fusion.13), channel_id=1, source_target_pairs={{0,32},{32,64},{64,96},{96,128},{128,160},{160,192},{192,224},{224... | collective-permute-start | bytes 884744 | tf_op jit(solution)/shard_map/ppermute | solution.py:137
  87.6 5.1 %collective-permute-start.10 = (f32[3,6,16,128]{3,2,1,0:T(8,128)S(1)}, f32[3,6,16,128]{3,2,1,0:T(8,128)S(1)}, u32[]{:S(2)}, u32[]{:S(2)}) collective-permute-start(f32[3,6,16,128]{3,2,1,0:T(8,128)S(1)} %multiply_subtract_fusion.2), channel_id=1, source_target_pairs={{0,960},{32,992},{64,0},{96,32},{128,64},{160,96},{192,128},{224,1... | collective-permute-start | bytes 442376 | tf_op jit(solution)/shard_map/ppermute | solution.py:138
  92.8 2.3 %collective-permute-done.8 = f32[6,6,16,128]{3,2,1,0:T(8,128)S(1)} collective-permute-done((f32[6,6,16,128]{3,2,1,0:T(8,128)S(1)}, f32[6,6,16,128]{3,2,1,0:T(8,128)S(1)}, u32[]{:S(2)}, u32[]{:S(2)}) %collective-permute-start.8) | collective-permute-done | bytes 294944 | tf_op jit(solution)/shard_map/ppermute | solution.py:137
  95.2 3.1 %collective-permute-done.11 = f32[3,6,16,128]{3,2,1,0:T(8,128)S(1)} collective-permute-done((f32[3,6,16,128]{3,2,1,0:T(8,128)S(1)}, f32[3,6,16,128]{3,2,1,0:T(8,128)S(1)}, u32[]{:S(2)}, u32[]{:S(2)}) %collective-permute-start.11) | collective-permute-done | bytes 147488 | tf_op jit(solution)/shard_map/ppermute | solution.py:137
  102.8 4.8 %collective-permute-start.12 = (f32[6,6,16,128]{3,2,1,0:T(8,128)S(1)}, f32[6,6,16,128]{3,2,1,0:T(8,128)S(1)}, u32[]{:S(2)}, u32[]{:S(2)}) collective-permute-start(f32[6,6,16,128]{3,2,1,0:T(8,128)S(1)} %pad_maximum_fusion.14), channel_id=1, source_target_pairs={{0,32},{32,64},{64,96},{96,128},{128,160},{160,192},{192,224},{224... | collective-permute-start | bytes 884744 | tf_op jit(solution)/shard_map/ppermute | solution.py:137
  109.5 5.1 %collective-permute-start.14 = (f32[3,6,16,128]{3,2,1,0:T(8,128)S(1)}, f32[3,6,16,128]{3,2,1,0:T(8,128)S(1)}, u32[]{:S(2)}, u32[]{:S(2)}) collective-permute-start(f32[3,6,16,128]{3,2,1,0:T(8,128)S(1)} %multiply_subtract_fusion.1), channel_id=1, source_target_pairs={{0,960},{32,992},{64,0},{96,32},{128,64},{160,96},{192,128},{224,1... | collective-permute-start | bytes 442376 | tf_op jit(solution)/shard_map/ppermute | solution.py:138
  114.7 2.8 %collective-permute-done.12 = f32[6,6,16,128]{3,2,1,0:T(8,128)S(1)} collective-permute-done((f32[6,6,16,128]{3,2,1,0:T(8,128)S(1)}, f32[6,6,16,128]{3,2,1,0:T(8,128)S(1)}, u32[]{:S(2)}, u32[]{:S(2)}) %collective-permute-start.12) | collective-permute-done | bytes 294944 | tf_op jit(solution)/shard_map/ppermute | solution.py:137
  117.6 2.2 %collective-permute-done.15 = f32[3,6,16,128]{3,2,1,0:T(8,128)S(1)} collective-permute-done((f32[3,6,16,128]{3,2,1,0:T(8,128)S(1)}, f32[3,6,16,128]{3,2,1,0:T(8,128)S(1)}, u32[]{:S(2)}, u32[]{:S(2)}) %collective-permute-start.15) | collective-permute-done | bytes 147488 | tf_op jit(solution)/shard_map/ppermute | solution.py:137
  124.3 3.9 %collective-permute-start.16 = (f32[3,6,16,128]{3,2,1,0:T(8,128)S(1)}, f32[3,6,16,128]{3,2,1,0:T(8,128)S(1)}, u32[]{:S(2)}, u32[]{:S(2)}) collective-permute-start(f32[3,6,16,128]{3,2,1,0:T(8,128)S(1)} %multiply_subtract_fusion), channel_id=1, source_target_pairs={{0,992},{32,0},{64,32},{96,64},{128,96},{160,128},{192,160},{224,1... | collective-permute-start | bytes 442376 | tf_op jit(solution)/shard_map/ppermute | solution.py:138
  128.4 4.2 %collective-permute-done.17 = f32[3,6,16,128]{3,2,1,0:T(8,128)S(1)} collective-permute-done((f32[3,6,16,128]{3,2,1,0:T(8,128)S(1)}, f32[3,6,16,128]{3,2,1,0:T(8,128)S(1)}, u32[]{:S(2)}, u32[]{:S(2)}) %collective-permute-start.17) | collective-permute-done | bytes 147488 | tf_op jit(solution)/shard_map/ppermute | solution.py:137
  133.3 18.4 %all_to_all.21 = f32[32,6,384]{2,1,0:T(8,128)S(1)} all-to-all(f32[32,6,384]{2,1,0:T(8,128)S(1)} %maximum_bitcast_fusion), channel_id=1, replica_groups=mesh['domain'=32,'band'=32] {'band'}, dimensions={0} | all-to-all | bytes 589824 | tf_op jit(solution)/shard_map/all_to_all | solution.py:114
  152.6 14.5 %all_to_all.22 = f32[32,2,3,96]{3,1,2,0:T(2,128)S(1)} all-to-all(f32[32,2,3,96]{3,1,2,0:T(2,128)S(1)} %copy.42), channel_id=1, replica_groups=mesh['domain'=32,'band'=32] {'band'}, dimensions={0} | all-to-all | bytes 147456 | tf_op jit(solution)/shard_map/all_to_all | solution.py:120
  167.2 21.9 %all_to_all.23 = f32[32,2,3,96]{3,1,2,0:T(2,128)S(1)} all-to-all(f32[32,2,3,96]{3,1,2,0:T(2,128)S(1)} %broadcast_in_dim.5), channel_id=1, replica_groups=mesh['domain'=32,'band'=32] {'domain'}, dimensions={0} | all-to-all | bytes 147456 | tf_op jit(solution)/shard_map/all_to_all | solution.py:124
  (83 shorter events, 28.0 us)
Async XLA Ops:
  0.6 0.7 copy-start
  22.0 0.9 copy-start.1
  23.0 28.3 %collective-permute-start.1 = (f32[4,6,16,128]{3,2,1,0:T(8,128)S(1)}, f32[4,6,16,128]{3,2,1,0:T(8,128)S(1)}, u32[]{:S(2)}, u32[]{:S(2)}) collective-permute-start(f32[4,6,16,128]{3,2,1,0:T(8,128)S(1)} %pad_maximum_fusion.15), channel_id=1, source_target_pairs={{0,992},{32,0},{64,32},{96,64},{128,96},{160,128},{192,160},{224,1... | collective-permute-start | bytes 589832 | tf_op jit(solution)/shard_map/ppermute | solution.py:138
  32.2 19.1 %collective-permute-start = (f32[4,6,16,128]{3,2,1,0:T(8,128)S(1)}, f32[4,6,16,128]{3,2,1,0:T(8,128)S(1)}, u32[]{:S(2)}, u32[]{:S(2)}) collective-permute-start(f32[4,6,16,128]{3,2,1,0:T(8,128)S(1)} %pad_maximum_fusion.15), channel_id=1, source_target_pairs={{0,32},{32,64},{64,96},{96,128},{128,160},{160,192},{192,224},{224... | collective-permute-start | bytes 589832 | tf_op jit(solution)/shard_map/ppermute | solution.py:137
  34.1 20.9 %collective-permute-start.3 = (f32[3,6,16,128]{3,2,1,0:T(8,128)S(1)}, f32[3,6,16,128]{3,2,1,0:T(8,128)S(1)}, u32[]{:S(2)}, u32[]{:S(2)}) collective-permute-start(f32[3,6,16,128]{3,2,1,0:T(8,128)S(1)} %copy-done.1), channel_id=1, source_target_pairs={{0,64},{32,96},{64,128},{96,160},{128,192},{160,224},{192,256},{22... | collective-permute-start | bytes 442376 | tf_op jit(solution)/shard_map/ppermute | solution.py:137
  36.0 19.0 %collective-permute-start.2 = (f32[3,6,16,128]{3,2,1,0:T(8,128)S(1)}, f32[3,6,16,128]{3,2,1,0:T(8,128)S(1)}, u32[]{:S(2)}, u32[]{:S(2)}) collective-permute-start(f32[3,6,16,128]{3,2,1,0:T(8,128)S(1)} %copy-done.1), channel_id=1, source_target_pairs={{0,960},{32,992},{64,0},{96,32},{128,64},{160,96},{192,128},{224,1... | collective-permute-start | bytes 442376 | tf_op jit(solution)/shard_map/ppermute | solution.py:138
  57.5 14.4 %collective-permute-start.5 = (f32[6,6,16,128]{3,2,1,0:T(8,128)S(1)}, f32[6,6,16,128]{3,2,1,0:T(8,128)S(1)}, u32[]{:S(2)}, u32[]{:S(2)}) collective-permute-start(f32[6,6,16,128]{3,2,1,0:T(8,128)S(1)} %pad_maximum_fusion.12), channel_id=1, source_target_pairs={{0,992},{32,0},{64,32},{96,64},{128,96},{160,128},{192,160},{224,1... | collective-permute-start | bytes 884744 | tf_op jit(solution)/shard_map/ppermute | solution.py:138
  59.4 15.1 %collective-permute-start.4 = (f32[6,6,16,128]{3,2,1,0:T(8,128)S(1)}, f32[6,6,16,128]{3,2,1,0:T(8,128)S(1)}, u32[]{:S(2)}, u32[]{:S(2)}) collective-permute-start(f32[6,6,16,128]{3,2,1,0:T(8,128)S(1)} %pad_maximum_fusion.12), channel_id=1, source_target_pairs={{0,32},{32,64},{64,96},{96,128},{128,160},{160,192},{192,224},{224... | collective-permute-start | bytes 884744 | tf_op jit(solution)/shard_map/ppermute | solution.py:137
  64.2 12.2 %collective-permute-start.7 = (f32[3,6,16,128]{3,2,1,0:T(8,128)S(1)}, f32[3,6,16,128]{3,2,1,0:T(8,128)S(1)}, u32[]{:S(2)}, u32[]{:S(2)}) collective-permute-start(f32[3,6,16,128]{3,2,1,0:T(8,128)S(1)} %multiply_subtract_fusion.3), channel_id=1, source_target_pairs={{0,64},{32,96},{64,128},{96,160},{128,192},{160,224},{192,256},{22... | collective-permute-start | bytes 442376 | tf_op jit(solution)/shard_map/ppermute | solution.py:137
  66.1 10.3 %collective-permute-start.6 = (f32[3,6,16,128]{3,2,1,0:T(8,128)S(1)}, f32[3,6,16,128]{3,2,1,0:T(8,128)S(1)}, u32[]{:S(2)}, u32[]{:S(2)}) collective-permute-start(f32[3,6,16,128]{3,2,1,0:T(8,128)S(1)} %multiply_subtract_fusion.3), channel_id=1, source_target_pairs={{0,960},{32,992},{64,0},{96,32},{128,64},{160,96},{192,128},{224,1... | collective-permute-start | bytes 442376 | tf_op jit(solution)/shard_map/ppermute | solution.py:138
  79.0 13.8 %collective-permute-start.9 = (f32[6,6,16,128]{3,2,1,0:T(8,128)S(1)}, f32[6,6,16,128]{3,2,1,0:T(8,128)S(1)}, u32[]{:S(2)}, u32[]{:S(2)}) collective-permute-start(f32[6,6,16,128]{3,2,1,0:T(8,128)S(1)} %pad_maximum_fusion.13), channel_id=1, source_target_pairs={{0,992},{32,0},{64,32},{96,64},{128,96},{160,128},{192,160},{224,1... | collective-permute-start | bytes 884744 | tf_op jit(solution)/shard_map/ppermute | solution.py:138
  80.9 14.2 %collective-permute-start.8 = (f32[6,6,16,128]{3,2,1,0:T(8,128)S(1)}, f32[6,6,16,128]{3,2,1,0:T(8,128)S(1)}, u32[]{:S(2)}, u32[]{:S(2)}) collective-permute-start(f32[6,6,16,128]{3,2,1,0:T(8,128)S(1)} %pad_maximum_fusion.13), channel_id=1, source_target_pairs={{0,32},{32,64},{64,96},{96,128},{128,160},{160,192},{192,224},{224... | collective-permute-start | bytes 884744 | tf_op jit(solution)/shard_map/ppermute | solution.py:137
  85.7 12.6 %collective-permute-start.11 = (f32[3,6,16,128]{3,2,1,0:T(8,128)S(1)}, f32[3,6,16,128]{3,2,1,0:T(8,128)S(1)}, u32[]{:S(2)}, u32[]{:S(2)}) collective-permute-start(f32[3,6,16,128]{3,2,1,0:T(8,128)S(1)} %multiply_subtract_fusion.2), channel_id=1, source_target_pairs={{0,64},{32,96},{64,128},{96,160},{128,192},{160,224},{192,256},{22... | collective-permute-start | bytes 442376 | tf_op jit(solution)/shard_map/ppermute | solution.py:137
  87.6 10.7 %collective-permute-start.10 = (f32[3,6,16,128]{3,2,1,0:T(8,128)S(1)}, f32[3,6,16,128]{3,2,1,0:T(8,128)S(1)}, u32[]{:S(2)}, u32[]{:S(2)}) collective-permute-start(f32[3,6,16,128]{3,2,1,0:T(8,128)S(1)} %multiply_subtract_fusion.2), channel_id=1, source_target_pairs={{0,960},{32,992},{64,0},{96,32},{128,64},{160,96},{192,128},{224,1... | collective-permute-start | bytes 442376 | tf_op jit(solution)/shard_map/ppermute | solution.py:138
  100.8 13.8 %collective-permute-start.13 = (f32[6,6,16,128]{3,2,1,0:T(8,128)S(1)}, f32[6,6,16,128]{3,2,1,0:T(8,128)S(1)}, u32[]{:S(2)}, u32[]{:S(2)}) collective-permute-start(f32[6,6,16,128]{3,2,1,0:T(8,128)S(1)} %pad_maximum_fusion.14), channel_id=1, source_target_pairs={{0,992},{32,0},{64,32},{96,64},{128,96},{160,128},{192,160},{224,1... | collective-permute-start | bytes 884744 | tf_op jit(solution)/shard_map/ppermute | solution.py:138
  102.8 14.7 %collective-permute-start.12 = (f32[6,6,16,128]{3,2,1,0:T(8,128)S(1)}, f32[6,6,16,128]{3,2,1,0:T(8,128)S(1)}, u32[]{:S(2)}, u32[]{:S(2)}) collective-permute-start(f32[6,6,16,128]{3,2,1,0:T(8,128)S(1)} %pad_maximum_fusion.14), channel_id=1, source_target_pairs={{0,32},{32,64},{64,96},{96,128},{128,160},{160,192},{192,224},{224... | collective-permute-start | bytes 884744 | tf_op jit(solution)/shard_map/ppermute | solution.py:137
  107.6 12.2 %collective-permute-start.15 = (f32[3,6,16,128]{3,2,1,0:T(8,128)S(1)}, f32[3,6,16,128]{3,2,1,0:T(8,128)S(1)}, u32[]{:S(2)}, u32[]{:S(2)}) collective-permute-start(f32[3,6,16,128]{3,2,1,0:T(8,128)S(1)} %multiply_subtract_fusion.1), channel_id=1, source_target_pairs={{0,64},{32,96},{64,128},{96,160},{128,192},{160,224},{192,256},{22... | collective-permute-start | bytes 442376 | tf_op jit(solution)/shard_map/ppermute | solution.py:137
  109.5 10.3 %collective-permute-start.14 = (f32[3,6,16,128]{3,2,1,0:T(8,128)S(1)}, f32[3,6,16,128]{3,2,1,0:T(8,128)S(1)}, u32[]{:S(2)}, u32[]{:S(2)}) collective-permute-start(f32[3,6,16,128]{3,2,1,0:T(8,128)S(1)} %multiply_subtract_fusion.1), channel_id=1, source_target_pairs={{0,960},{32,992},{64,0},{96,32},{128,64},{160,96},{192,128},{224,1... | collective-permute-start | bytes 442376 | tf_op jit(solution)/shard_map/ppermute | solution.py:138
  122.3 10.7 %copy-start.2 = (f32[3,6,16,128]{3,2,1,0:T(8,128)}, f32[3,6,16,128]{3,2,1,0:T(8,128)S(1)}, u32[]{:S(2)}) copy-start(f32[3,6,16,128]{3,2,1,0:T(8,128)S(1)} %multiply_subtract_fusion) | copy-start | bytes 442372
  122.4 10.2 %collective-permute-start.17 = (f32[3,6,16,128]{3,2,1,0:T(8,128)S(1)}, f32[3,6,16,128]{3,2,1,0:T(8,128)S(1)}, u32[]{:S(2)}, u32[]{:S(2)}) collective-permute-start(f32[3,6,16,128]{3,2,1,0:T(8,128)S(1)} %multiply_subtract_fusion), channel_id=1, source_target_pairs={{0,32},{32,64},{64,96},{96,128},{128,160},{160,192},{192,224},{224... | collective-permute-start | bytes 442376 | tf_op jit(solution)/shard_map/ppermute | solution.py:137
  124.3 8.3 %collective-permute-start.16 = (f32[3,6,16,128]{3,2,1,0:T(8,128)S(1)}, f32[3,6,16,128]{3,2,1,0:T(8,128)S(1)}, u32[]{:S(2)}, u32[]{:S(2)}) collective-permute-start(f32[3,6,16,128]{3,2,1,0:T(8,128)S(1)} %multiply_subtract_fusion), channel_id=1, source_target_pairs={{0,992},{32,0},{64,32},{96,64},{128,96},{160,128},{192,160},{224,1... | collective-permute-start | bytes 442376 | tf_op jit(solution)/shard_map/ppermute | solution.py:138
